TPU v7x, 32 devices: a whole 2x2x4 slice. The times are simulated.
32 devices in a mesh: section: 4 (over y, x), expert: 8 (over z, core).
Axes of the slice: x: 2, y: 2, z: 4, core: 2. Of those that a mesh axis runs over, the one named last changes fastest.
Arguments:
- tokens: bfloat16 [4, 128, 2048], P(None, 'expert'), may hold values from -6 to 6
- norm_gain: float32 [4, 2048], P('section'), may hold values from 0.1 to 1.9
- gate_weight: bfloat16 [4, 16, 2048, 768], P('section', 'expert'), may hold values from -0.125 to 0.125
- up_weight: bfloat16 [4, 16, 2048, 768], P('section', 'expert'), may hold values from -0.125 to 0.125
- down_weight: bfloat16 [4, 16, 768, 2048], P('section', 'expert'), may hold values from -0.21875 to 0.21875
- routes: int32 [4, 4, 128, 8], P('section', None, 'expert'), may hold values from 0 to 15, all different within a row; in each aligned block of 16 rows (0 to 15, 16 to 31, ..., all dimensions but the last counted through in order) at most 12 rows name the same one
- gates: float32 [4, 4, 128, 8], P('section', None, 'expert'), may hold values from 0.1 to 1
Outputs:
- hidden_states: bfloat16 [4, 4, 128, 2048], P('section', None, 'expert')
Inputs may be any that keep to these rules, and one draw needn't show every extreme that they name: `routes`: within one section and micro-batch, the 16 tokens of one device name any one expert at most 12 times, a bound that some expert reaches in some of these blocks; the 8 experts of a token differ.
All inputs are finite; a program needn't handle non-finite values.
Results may differ from a plain program's by a relative error of at most 0.012.
Values may be sent and summed in bfloat16 or wider, within the bound.
No kernel may reach another device: no remote copies, remote signals or barrier semaphores. Data moves between devices by JAX's collectives and lax.ppermute only.
A program may use at most 128 MiB of HBM per device.

v0:
```python
import jax
import jax.numpy as jnp
from jax import lax
from jax.sharding import PartitionSpec as P

MB = 4
EPSILON = 1e-06


def shifted(array, axis, by):
    count = lax.axis_size(axis)
    pairs = [(i, i + by) for i in range(count) if 0 <= i + by < count]
    return lax.ppermute(array, axis, pairs)


def place_slots(expert_ids, experts):
    onehot = (expert_ids[:, None] == jnp.arange(experts, dtype=jnp.int32)[None, :]).astype(
        jnp.int32
    )
    before = jnp.cumsum(onehot, axis=0) - onehot
    return jnp.sum(before * onehot, axis=1)


def rms_normed(hidden, gain):
    values = hidden.astype(jnp.float32)
    scale = lax.rsqrt(jnp.mean(values * values, axis=-1, keepdims=True) + EPSILON)
    return (values, (values * scale * gain).astype(jnp.bfloat16))


def on_device(tokens, norm_gain, gate_weight, up_weight, down_weight, routes, gates):
    devices = lax.axis_size("expert")
    sections = lax.axis_size("section")
    section_index = lax.axis_index("section")
    local_experts = gate_weight.shape[1]
    experts = local_experts * devices
    tok_rows = tokens.shape[1]
    width = tokens.shape[2]
    topk = routes.shape[3]
    capacity = tok_rows * topk * 3 // (2 * experts)
    gain = norm_gain[0]
    w_gate = gate_weight[0]
    w_up = up_weight[0]
    w_down = down_weight[0]
    held = jnp.zeros((tok_rows, width), jnp.bfloat16)
    collected = jnp.zeros((MB, tok_rows, width), jnp.bfloat16)
    for moment in range(MB + sections - 1):
        if moment > 0:
            arrived = shifted(held, "section", 1)
        else:
            arrived = held
        batch_index = moment - section_index
        active = (batch_index >= 0) & (batch_index < MB)
        clipped = jnp.clip(batch_index, 0, MB - 1)
        first_rows = lax.dynamic_index_in_dim(tokens, clipped, 0, keepdims=False)
        incoming = jnp.where(section_index == 0, first_rows, arrived)
        expert_ids = lax.dynamic_index_in_dim(routes[0], clipped, 0, keepdims=False)
        gate_values = lax.dynamic_index_in_dim(gates[0], clipped, 0, keepdims=False)
        values, normed = rms_normed(incoming, gain)
        flat_ids = expert_ids.reshape(-1)
        slot_index = place_slots(flat_ids, experts)
        token_index = jnp.arange(tok_rows * topk, dtype=jnp.int32) // topk
        outgoing = jnp.zeros((experts, capacity, width), jnp.bfloat16)
        outgoing = outgoing.at[flat_ids, slot_index].set(normed[token_index])
        outgoing = outgoing.reshape(devices, local_experts, capacity, width)
        received = lax.all_to_all(outgoing, "expert", split_axis=0, concat_axis=0, tiled=True)
        gate_part = jnp.einsum(
            "nesd,edf->nesf", received, w_gate, preferred_element_type=jnp.float32
        )
        up_part = jnp.einsum("nesd,edf->nesf", received, w_up, preferred_element_type=jnp.float32)
        inner = (jax.nn.silu(gate_part) * up_part).astype(jnp.bfloat16)
        returned = lax.all_to_all(
            jnp.einsum("nesf,efd->nesd", inner, w_down, preferred_element_type=jnp.float32).astype(
                jnp.bfloat16
            ),
            "expert",
            split_axis=0,
            concat_axis=0,
            tiled=True,
        )
        returned = returned.reshape(experts, capacity, width)
        picked = returned[flat_ids, slot_index].reshape(tok_rows, topk, width)
        weights = gate_values / jnp.sum(gate_values, axis=-1, keepdims=True)
        mixed = jnp.sum(weights[:, :, None] * picked.astype(jnp.float32), axis=1)
        produced = (values + mixed).astype(jnp.bfloat16)
        held = jnp.where(active, produced, incoming)
        updated = lax.dynamic_update_index_in_dim(collected, held, clipped, 0)
        collected = jnp.where(active, updated, collected)
    return collected[None]


def solution(mesh):
    placed = (
        P(None, "expert", None),
        P("section", None),
        P("section", "expert", None, None),
        P("section", "expert", None, None),
        P("section", "expert", None, None),
        P("section", None, "expert", None),
        P("section", None, "expert", None),
    )
    return jax.shard_map(
        on_device,
        mesh=mesh,
        in_specs=placed,
        out_specs=P("section", None, "expert", None),
        check_vma=False,
    )
```

profile of v0, /device:TPU:4, one launch (start us, length us, event | category | flops | bytes accessed | tf_op | source)
XLA Modules:
  0.0 598.4 jit_solution(2576998763865678790)
XLA Ops:
  5.2 11.8 %scatter_fusion = bf16[16,12,2048]{2,0,1:T(8,128)(2,1)S(1)} fusion(bf16[16,12,2048]{2,0,1:T(8,128)(2,1)S(1)} %broadcast.475.clone, s32[128]{0:T(128)S(1)} %get-tuple-element.46, bf16[128,2048]{1,0:T(8,128)(2,1)S(1)} %gather_fusion), kind=kCustom, calls=%fused_computation.14 | custom fusion | bytes 1573888 | tf_op jit(solution)/shard_map/scatter | solution.py:63
  18.1 25.7 %all_to_all.70 = bf16[8,2,12,2048]{3,1,2,0:T(2,128)(2,1)S(1)} all-to-all(bf16[8,2,12,2048]{3,1,2,0:T(2,128)(2,1)S(1)} %copy.67), channel_id=1, replica_groups=mesh['section'=4,'expert'=8] {'expert'}, dimensions={0} | all-to-all | bytes 1572864 | tf_op jit(solution)/shard_map/all_to_all | solution.py:65
  43.8 3.9 fusion.84
  47.8 6.8 %fusion.81 = bf16[8,2,12,2048]{3,2,0,1:T(8,128)(2,1)S(1)} fusion(bf16[1,2,768,2048]{3,2,1,0:T(8,128)(2,1)} %param.11, bf16[1,2,2048,768]{3,2,1,0:T(8,128)(2,1)} %param.10, bf16[8,2,12,2048]{3,1,2,0:T(2,128)(2,1)S(1)} %all_to_all.70, f32[8,2,12,768]{3,2,0,1:T(8,128)S(1)} %fusion.84), kind=kOutput, calls=%fused_computation.76 | convolution fusion | flops 1209237504 | bytes 14745600 | tf_op jit(solution)/shard_map/nesf,efd->nesd/dot_general | solution.py:72
  54.6 1.7 copy.70
  56.2 3.5 all-to-all-start.1
  60.0 20.7 %all-to-all-done.1 = bf16[8,2,12,2048]{3,1,2,0:T(2,128)(2,1)S(1)} async-done(((bf16[8,2,12,2048]{3,1,2,0:T(2,128)(2,1)}), bf16[8,2,12,2048]{3,1,2,0:T(2,128)(2,1)S(1)}, u32[]{:S(2)}, u32[]{:S(2)}) %all-to-all-start.1) | async-done | bytes 786464 | tf_op jit(solution)/shard_map/all_to_all | solution.py:71
  81.7 2.4 gather_fusion.1
  84.6 3.9 collective-permute-start
  88.5 3.2 collective-permute-done
  92.9 11.8 %scatter_fusion.1 = bf16[16,12,2048]{2,0,1:T(8,128)(2,1)S(1)} fusion(bf16[16,12,2048]{2,0,1:T(8,128)(2,1)S(1)} %broadcast.475.clone.1, s32[128]{0:T(128)S(1)} %get-tuple-element.62, bf16[128,2048]{1,0:T(8,128)(2,1)S(1)} %gather_fusion.2), kind=kCustom, calls=%fused_computation.15 | custom fusion | bytes 1573888 | tf_op jit(solution)/shard_map/scatter | solution.py:63
  105.9 23.4 %all_to_all.71 = bf16[8,2,12,2048]{3,1,2,0:T(2,128)(2,1)S(1)} all-to-all(bf16[8,2,12,2048]{3,1,2,0:T(2,128)(2,1)S(1)} %copy.75), channel_id=1, replica_groups=mesh['section'=4,'expert'=8] {'expert'}, dimensions={0} | all-to-all | bytes 1572864 | tf_op jit(solution)/shard_map/all_to_all | solution.py:65
  129.3 3.9 fusion.87
  133.2 6.7 %fusion.78 = bf16[8,2,12,2048]{3,2,0,1:T(8,128)(2,1)S(1)} fusion(bf16[1,2,768,2048]{3,2,1,0:T(8,128)(2,1)} %param.11, bf16[1,2,2048,768]{3,2,1,0:T(8,128)(2,1)} %param.10, bf16[8,2,12,2048]{3,1,2,0:T(2,128)(2,1)S(1)} %all_to_all.71, f32[8,2,12,768]{3,2,0,1:T(8,128)S(1)} %fusion.87), kind=kOutput, calls=%fused_computation.75 | convolution fusion | flops 1209237504 | bytes 14745600 | tf_op jit(solution)/shard_map/nesf,efd->nesd/dot_general | solution.py:72
  140.0 1.7 copy.78
  141.7 3.5 all-to-all-start.3
  146.8 19.3 %all-to-all-done.3 = bf16[8,2,12,2048]{3,1,2,0:T(2,128)(2,1)S(1)} async-done(((bf16[8,2,12,2048]{3,1,2,0:T(2,128)(2,1)}), bf16[8,2,12,2048]{3,1,2,0:T(2,128)(2,1)S(1)}, u32[]{:S(2)}, u32[]{:S(2)}) %all-to-all-start.3) | async-done | bytes 786464 | tf_op jit(solution)/shard_map/all_to_all | solution.py:71
  167.1 2.4 gather_fusion.3
  170.0 2.7 collective-permute-start.1
  172.8 4.3 collective-permute-done.1
  178.4 11.8 %scatter_fusion.2 = bf16[16,12,2048]{2,0,1:T(8,128)(2,1)S(1)} fusion(bf16[16,12,2048]{2,0,1:T(8,128)(2,1)S(1)} %broadcast.475.clone.2, s32[128]{0:T(128)S(1)} %get-tuple-element.38, bf16[128,2048]{1,0:T(8,128)(2,1)S(1)} %gather_fusion.4), kind=kCustom, calls=%fused_computation.16 | custom fusion | bytes 1573888 | tf_op jit(solution)/shard_map/scatter | solution.py:63
  191.3 23.4 %all_to_all.72 = bf16[8,2,12,2048]{3,1,2,0:T(2,128)(2,1)S(1)} all-to-all(bf16[8,2,12,2048]{3,1,2,0:T(2,128)(2,1)S(1)} %copy.83), channel_id=1, replica_groups=mesh['section'=4,'expert'=8] {'expert'}, dimensions={0} | all-to-all | bytes 1572864 | tf_op jit(solution)/shard_map/all_to_all | solution.py:65
  214.7 3.9 fusion.90
  218.6 6.8 %fusion.75 = bf16[8,2,12,2048]{3,2,0,1:T(8,128)(2,1)S(1)} fusion(bf16[1,2,768,2048]{3,2,1,0:T(8,128)(2,1)} %param.11, bf16[1,2,2048,768]{3,2,1,0:T(8,128)(2,1)} %param.10, bf16[8,2,12,2048]{3,1,2,0:T(2,128)(2,1)S(1)} %all_to_all.72, f32[8,2,12,768]{3,2,0,1:T(8,128)S(1)} %fusion.90), kind=kOutput, calls=%fused_computation.74 | convolution fusion | flops 1209237504 | bytes 14745600 | tf_op jit(solution)/shard_map/nesf,efd->nesd/dot_general | solution.py:72
  227.1 3.5 all-to-all-start.5
  230.8 20.8 %all-to-all-done.5 = bf16[8,2,12,2048]{3,1,2,0:T(2,128)(2,1)S(1)} async-done(((bf16[8,2,12,2048]{3,1,2,0:T(2,128)(2,1)}), bf16[8,2,12,2048]{3,1,2,0:T(2,128)(2,1)S(1)}, u32[]{:S(2)}, u32[]{:S(2)}) %all-to-all-start.5) | async-done | bytes 786464 | tf_op jit(solution)/shard_map/all_to_all | solution.py:71
  252.6 2.4 gather_fusion.5
  255.5 2.1 collective-permute-start.2
  257.6 4.9 collective-permute-done.2
  263.8 11.8 %scatter_fusion.3 = bf16[16,12,2048]{2,0,1:T(8,128)(2,1)S(1)} fusion(bf16[16,12,2048]{2,0,1:T(8,128)(2,1)S(1)} %broadcast.475.clone.3, s32[128]{0:T(128)S(1)} %get-tuple-element.64, bf16[128,2048]{1,0:T(8,128)(2,1)S(1)} %gather_fusion.6), kind=kCustom, calls=%fused_computation.17 | custom fusion | bytes 1573888 | tf_op jit(solution)/shard_map/scatter | solution.py:63
  276.8 23.4 %all_to_all.73 = bf16[8,2,12,2048]{3,1,2,0:T(2,128)(2,1)S(1)} all-to-all(bf16[8,2,12,2048]{3,1,2,0:T(2,128)(2,1)S(1)} %copy.91), channel_id=1, replica_groups=mesh['section'=4,'expert'=8] {'expert'}, dimensions={0} | all-to-all | bytes 1572864 | tf_op jit(solution)/shard_map/all_to_all | solution.py:65
  300.2 3.9 fusion.93
  304.2 6.7 %fusion.72 = bf16[8,2,12,2048]{3,2,0,1:T(8,128)(2,1)S(1)} fusion(bf16[1,2,768,2048]{3,2,1,0:T(8,128)(2,1)} %param.11, bf16[1,2,2048,768]{3,2,1,0:T(8,128)(2,1)} %param.10, bf16[8,2,12,2048]{3,1,2,0:T(2,128)(2,1)S(1)} %all_to_all.73, f32[8,2,12,768]{3,2,0,1:T(8,128)S(1)} %fusion.93), kind=kOutput, calls=%fused_computation.73 | convolution fusion | flops 1209237504 | bytes 14745600 | tf_op jit(solution)/shard_map/nesf,efd->nesd/dot_general | solution.py:72
  312.6 3.5 all-to-all-start.7
  317.6 19.4 %all-to-all-done.7 = bf16[8,2,12,2048]{3,1,2,0:T(2,128)(2,1)S(1)} async-done(((bf16[8,2,12,2048]{3,1,2,0:T(2,128)(2,1)}), bf16[8,2,12,2048]{3,1,2,0:T(2,128)(2,1)S(1)}, u32[]{:S(2)}, u32[]{:S(2)}) %all-to-all-start.7) | async-done | bytes 786464 | tf_op jit(solution)/shard_map/all_to_all | solution.py:71
  338.0 2.4 gather_fusion.7
  341.0 2.3 collective-permute-start.3
  343.3 4.7 collective-permute-done.3
  349.3 11.9 %scatter_fusion.4 = bf16[16,12,2048]{2,0,1:T(8,128)(2,1)S(1)} fusion(bf16[16,12,2048]{2,0,1:T(8,128)(2,1)S(1)} %broadcast.475.clone.4, s32[128]{0:T(128)S(1)} %get-tuple-element.26, bf16[128,2048]{1,0:T(8,128)(2,1)S(1)} %gather_fusion.8), kind=kCustom, calls=%fused_computation.18 | custom fusion | bytes 1573888 | tf_op jit(solution)/shard_map/scatter | solution.py:63
  362.2 23.4 %all_to_all.74 = bf16[8,2,12,2048]{3,1,2,0:T(2,128)(2,1)S(1)} all-to-all(bf16[8,2,12,2048]{3,1,2,0:T(2,128)(2,1)S(1)} %copy.99), channel_id=1, replica_groups=mesh['section'=4,'expert'=8] {'expert'}, dimensions={0} | all-to-all | bytes 1572864 | tf_op jit(solution)/shard_map/all_to_all | solution.py:65
  385.6 3.9 fusion.96
  389.6 6.8 %fusion.69 = bf16[8,2,12,2048]{3,2,0,1:T(8,128)(2,1)S(1)} fusion(bf16[1,2,768,2048]{3,2,1,0:T(8,128)(2,1)} %param.11, bf16[1,2,2048,768]{3,2,1,0:T(8,128)(2,1)} %param.10, bf16[8,2,12,2048]{3,1,2,0:T(2,128)(2,1)S(1)} %all_to_all.74, f32[8,2,12,768]{3,2,0,1:T(8,128)S(1)} %fusion.96), kind=kOutput, calls=%fused_computation.72 | convolution fusion | flops 1209237504 | bytes 14745600 | tf_op jit(solution)/shard_map/nesf,efd->nesd/dot_general | solution.py:72
  396.4 1.7 copy.102
  398.1 3.5 all-to-all-start.9
  401.7 20.8 %all-to-all-done.9 = bf16[8,2,12,2048]{3,1,2,0:T(2,128)(2,1)S(1)} async-done(((bf16[8,2,12,2048]{3,1,2,0:T(2,128)(2,1)}), bf16[8,2,12,2048]{3,1,2,0:T(2,128)(2,1)S(1)}, u32[]{:S(2)}, u32[]{:S(2)}) %all-to-all-start.9) | async-done | bytes 786464 | tf_op jit(solution)/shard_map/all_to_all | solution.py:71
  423.5 2.4 gather_fusion.9
  426.4 2.1 collective-permute-start.4
  428.5 5.0 collective-permute-done.4
  434.8 11.8 %scatter_fusion.5 = bf16[16,12,2048]{2,0,1:T(8,128)(2,1)S(1)} fusion(bf16[16,12,2048]{2,0,1:T(8,128)(2,1)S(1)} %broadcast.475.clone.5, s32[128]{0:T(128)S(1)} %get-tuple-element.66, bf16[128,2048]{1,0:T(8,128)(2,1)S(1)} %gather_fusion.10), kind=kCustom, calls=%fused_computation.19 | custom fusion | bytes 1573888 | tf_op jit(solution)/shard_map/scatter | solution.py:63
  447.8 23.4 %all_to_all.75 = bf16[8,2,12,2048]{3,1,2,0:T(2,128)(2,1)S(1)} all-to-all(bf16[8,2,12,2048]{3,1,2,0:T(2,128)(2,1)S(1)} %copy.107), channel_id=1, replica_groups=mesh['section'=4,'expert'=8] {'expert'}, dimensions={0} | all-to-all | bytes 1572864 | tf_op jit(solution)/shard_map/all_to_all | solution.py:65
  471.2 4.0 fusion.99
  475.1 6.8 %fusion.66 = bf16[8,2,12,2048]{3,2,0,1:T(8,128)(2,1)S(1)} fusion(bf16[1,2,768,2048]{3,2,1,0:T(8,128)(2,1)} %param.11, bf16[1,2,2048,768]{3,2,1,0:T(8,128)(2,1)} %param.10, bf16[8,2,12,2048]{3,1,2,0:T(2,128)(2,1)S(1)} %all_to_all.75, f32[8,2,12,768]{3,2,0,1:T(8,128)S(1)} %fusion.99), kind=kOutput, calls=%fused_computation.71 | convolution fusion | flops 1209237504 | bytes 14745600 | tf_op jit(solution)/shard_map/nesf,efd->nesd/dot_general | solution.py:72
  483.6 3.5 all-to-all-start.11
  487.9 20.1 %all-to-all-done.11 = bf16[8,2,12,2048]{3,1,2,0:T(2,128)(2,1)S(1)} async-done(((bf16[8,2,12,2048]{3,1,2,0:T(2,128)(2,1)}), bf16[8,2,12,2048]{3,1,2,0:T(2,128)(2,1)S(1)}, u32[]{:S(2)}, u32[]{:S(2)}) %all-to-all-start.11) | async-done | bytes 786464 | tf_op jit(solution)/shard_map/all_to_all | solution.py:71
  509.0 2.4 gather_fusion.11
  512.0 2.1 collective-permute-start.5
  514.1 4.9 collective-permute-done.5
  520.3 11.8 %scatter_fusion.6 = bf16[16,12,2048]{2,0,1:T(8,128)(2,1)S(1)} fusion(bf16[16,12,2048]{2,0,1:T(8,128)(2,1)S(1)} %broadcast.475, s32[128]{0:T(128)S(1)} %get-tuple-element.14, bf16[128,2048]{1,0:T(8,128)(2,1)S(1)} %gather_fusion.12), kind=kCustom, calls=%fused_computation.20 | custom fusion | bytes 1573888 | tf_op jit(solution)/shard_map/scatter | solution.py:63
  533.3 23.4 %all_to_all.76 = bf16[8,2,12,2048]{3,1,2,0:T(2,128)(2,1)S(1)} all-to-all(bf16[8,2,12,2048]{3,1,2,0:T(2,128)(2,1)S(1)} %copy.115), channel_id=1, replica_groups=mesh['section'=4,'expert'=8] {'expert'}, dimensions={0} | all-to-all | bytes 1572864 | tf_op jit(solution)/shard_map/all_to_all | solution.py:65
  556.7 3.9 fusion.102
  560.6 6.8 %fusion.63 = bf16[8,2,12,2048]{3,2,0,1:T(8,128)(2,1)S(1)} fusion(bf16[1,2,768,2048]{3,2,1,0:T(8,128)(2,1)} %param.11, bf16[1,2,2048,768]{3,2,1,0:T(8,128)(2,1)} %param.10, bf16[8,2,12,2048]{3,1,2,0:T(2,128)(2,1)S(1)} %all_to_all.76, f32[8,2,12,768]{3,2,0,1:T(8,128)S(1)} %fusion.102), kind=kOutput, calls=%fused_computation.70 | convolution fusion | flops 1209237504 | bytes 14745600 | tf_op jit(solution)/shard_map/nesf,efd->nesd/dot_general | solution.py:72
  569.1 3.5 all-to-all-start.13
  573.5 20.1 %all-to-all-done.13 = bf16[8,2,12,2048]{3,1,2,0:T(2,128)(2,1)S(1)} async-done(((bf16[8,2,12,2048]{3,1,2,0:T(2,128)(2,1)}), bf16[8,2,12,2048]{3,1,2,0:T(2,128)(2,1)S(1)}, u32[]{:S(2)}, u32[]{:S(2)}) %all-to-all-start.13) | async-done | bytes 786464 | tf_op jit(solution)/shard_map/all_to_all | solution.py:71
  594.6 2.4 gather_fusion.13
  (148 shorter events, 42.6 us)
Async XLA Ops:
  47.8 12.0 %copy-start.2 = (f32[1,4,16,8]{2,3,1,0:T(8,128)S(1)}, f32[1,4,16,8]{2,3,1,0:T(8,128)}, u32[]{:S(2)}) copy-start(f32[1,4,16,8]{2,3,1,0:T(8,128)} %param.13) | copy-start | bytes 6148
  54.5 30.0 %copy-start = (bf16[4,16,2048]{2,1,0:T(8,128)(2,1)S(1)}, bf16[4,16,2048]{2,1,0:T(8,128)(2,1)}, u32[]{:S(2)}) copy-start(bf16[4,16,2048]{2,1,0:T(8,128)(2,1)} %param.7) | copy-start | bytes 786436
  54.5 37.3 %copy-start.1 = (f32[1,2048]{1,0:T(1,128)S(1)}, f32[1,2048]{1,0:T(1,128)}, u32[]{:S(2)}) copy-start(f32[1,2048]{1,0:T(1,128)} %param.8) | copy-start | bytes 24580
  56.2 24.4 %all-to-all-start.1 = ((bf16[8,2,12,2048]{3,1,2,0:T(2,128)(2,1)}), bf16[8,2,12,2048]{3,1,2,0:T(2,128)(2,1)S(1)}, u32[]{:S(2)}, u32[]{:S(2)}) async-start(bf16[8,2,12,2048]{3,1,2,0:T(2,128)(2,1)} %copy.70), calls=%async_computation.1 | async-start | bytes 1572864 | tf_op jit(solution)/shard_map/all_to_all | solution.py:71
  84.6 7.1 %collective-permute-start = (bf16[16,2048]{1,0:T(8,128)(2,1)S(1)}, bf16[16,2048]{1,0:T(8,128)(2,1)S(1)}, u32[]{:S(2)}, u32[]{:S(2)}) collective-permute-start(bf16[16,2048]{1,0:T(8,128)(2,1)S(1)} %fusion.288), channel_id=1, source_target_pairs={{0,8},{8,16},{16,24},{1,9},{9,17},{17,25},{2,10},{10,18},{18,26},{... | collective-permute-start | bytes 196616 | tf_op jit(solution)/shard_map/ppermute | solution.py:13
  141.7 24.4 %all-to-all-start.3 = ((bf16[8,2,12,2048]{3,1,2,0:T(2,128)(2,1)}), bf16[8,2,12,2048]{3,1,2,0:T(2,128)(2,1)S(1)}, u32[]{:S(2)}, u32[]{:S(2)}) async-start(bf16[8,2,12,2048]{3,1,2,0:T(2,128)(2,1)} %copy.78), calls=%async_computation.3 | async-start | bytes 1572864 | tf_op jit(solution)/shard_map/all_to_all | solution.py:71
  170.0 7.1 %collective-permute-start.1 = (bf16[16,2048]{1,0:T(8,128)(2,1)S(1)}, bf16[16,2048]{1,0:T(8,128)(2,1)S(1)}, u32[]{:S(2)}, u32[]{:S(2)}) collective-permute-start(bf16[16,2048]{1,0:T(8,128)(2,1)S(1)} %get-tuple-element.41), channel_id=1, source_target_pairs={{0,8},{8,16},{16,24},{1,9},{9,17},{17,25},{2,10},{10,18},{18,26},{... | collective-permute-start | bytes 196616 | tf_op jit(solution)/shard_map/ppermute | solution.py:13
  227.1 24.4 %all-to-all-start.5 = ((bf16[8,2,12,2048]{3,1,2,0:T(2,128)(2,1)}), bf16[8,2,12,2048]{3,1,2,0:T(2,128)(2,1)S(1)}, u32[]{:S(2)}, u32[]{:S(2)}) async-start(bf16[8,2,12,2048]{3,1,2,0:T(2,128)(2,1)} %copy.86), calls=%async_computation.5 | async-start | bytes 1572864 | tf_op jit(solution)/shard_map/all_to_all | solution.py:71
  255.5 7.1 %collective-permute-start.2 = (bf16[16,2048]{1,0:T(8,128)(2,1)S(1)}, bf16[16,2048]{1,0:T(8,128)(2,1)S(1)}, u32[]{:S(2)}, u32[]{:S(2)}) collective-permute-start(bf16[16,2048]{1,0:T(8,128)(2,1)S(1)} %get-tuple-element.35), channel_id=1, source_target_pairs={{0,8},{8,16},{16,24},{1,9},{9,17},{17,25},{2,10},{10,18},{18,26},{... | collective-permute-start | bytes 196616 | tf_op jit(solution)/shard_map/ppermute | solution.py:13
  312.6 24.4 %all-to-all-start.7 = ((bf16[8,2,12,2048]{3,1,2,0:T(2,128)(2,1)}), bf16[8,2,12,2048]{3,1,2,0:T(2,128)(2,1)S(1)}, u32[]{:S(2)}, u32[]{:S(2)}) async-start(bf16[8,2,12,2048]{3,1,2,0:T(2,128)(2,1)} %copy.94), calls=%async_computation.7 | async-start | bytes 1572864 | tf_op jit(solution)/shard_map/all_to_all | solution.py:71
  341.0 7.1 %collective-permute-start.3 = (bf16[16,2048]{1,0:T(8,128)(2,1)S(1)}, bf16[16,2048]{1,0:T(8,128)(2,1)S(1)}, u32[]{:S(2)}, u32[]{:S(2)}) collective-permute-start(bf16[16,2048]{1,0:T(8,128)(2,1)S(1)} %get-tuple-element.29), channel_id=1, source_target_pairs={{0,8},{8,16},{16,24},{1,9},{9,17},{17,25},{2,10},{10,18},{18,26},{... | collective-permute-start | bytes 196616 | tf_op jit(solution)/shard_map/ppermute | solution.py:13
  398.1 24.4 %all-to-all-start.9 = ((bf16[8,2,12,2048]{3,1,2,0:T(2,128)(2,1)}), bf16[8,2,12,2048]{3,1,2,0:T(2,128)(2,1)S(1)}, u32[]{:S(2)}, u32[]{:S(2)}) async-start(bf16[8,2,12,2048]{3,1,2,0:T(2,128)(2,1)} %copy.102), calls=%async_computation.9 | async-start | bytes 1572864 | tf_op jit(solution)/shard_map/all_to_all | solution.py:71
  426.4 7.1 %collective-permute-start.4 = (bf16[16,2048]{1,0:T(8,128)(2,1)S(1)}, bf16[16,2048]{1,0:T(8,128)(2,1)S(1)}, u32[]{:S(2)}, u32[]{:S(2)}) collective-permute-start(bf16[16,2048]{1,0:T(8,128)(2,1)S(1)} %get-tuple-element.23), channel_id=1, source_target_pairs={{0,8},{8,16},{16,24},{1,9},{9,17},{17,25},{2,10},{10,18},{18,26},{... | collective-permute-start | bytes 196616 | tf_op jit(solution)/shard_map/ppermute | solution.py:13
  483.6 24.4 %all-to-all-start.11 = ((bf16[8,2,12,2048]{3,1,2,0:T(2,128)(2,1)}), bf16[8,2,12,2048]{3,1,2,0:T(2,128)(2,1)S(1)}, u32[]{:S(2)}, u32[]{:S(2)}) async-start(bf16[8,2,12,2048]{3,1,2,0:T(2,128)(2,1)} %copy.110), calls=%async_computation.11 | async-start | bytes 1572864 | tf_op jit(solution)/shard_map/all_to_all | solution.py:71
  512.0 7.1 %collective-permute-start.5 = (bf16[16,2048]{1,0:T(8,128)(2,1)S(1)}, bf16[16,2048]{1,0:T(8,128)(2,1)S(1)}, u32[]{:S(2)}, u32[]{:S(2)}) collective-permute-start(bf16[16,2048]{1,0:T(8,128)(2,1)S(1)} %get-tuple-element.17), channel_id=1, source_target_pairs={{0,8},{8,16},{16,24},{1,9},{9,17},{17,25},{2,10},{10,18},{18,26},{... | collective-permute-start | bytes 196616 | tf_op jit(solution)/shard_map/ppermute | solution.py:13
  569.1 24.4 %all-to-all-start.13 = ((bf16[8,2,12,2048]{3,1,2,0:T(2,128)(2,1)}), bf16[8,2,12,2048]{3,1,2,0:T(2,128)(2,1)S(1)}, u32[]{:S(2)}, u32[]{:S(2)}) async-start(bf16[8,2,12,2048]{3,1,2,0:T(2,128)(2,1)} %copy.118), calls=%async_computation.13 | async-start | bytes 1572864 | tf_op jit(solution)/shard_map/all_to_all | solution.py:71
where the time goes:
time: 608 us; the launch traced here: 598 us
  waiting for transfers between devices  168 us (28%)
  blocking collectives  166 us (27%)
  local copies, waits for them, and re-layouts  137 us (23%)
  matrix products  75 us (12%)
  starting transfers between devices  40.1 us (7%)
  other arithmetic  10.5 us (2%)
    all_to_all x7, blocking collectives, on_device(): lax.all_to_all(outgoing, 'expert', split_axis=0, concat_axis=0, tiled=True)  166 us
    all_to_all x7, waiting for transfers between devices, on_device(): lax.all_to_all(jnp.einsum('nesf,efd->nesd', inner, w_down, preferred_elem...  141 us
    scatter x7, local copies, waits for them, and re-layouts, on_device(): outgoing = outgoing.at[flat_ids, slot_index].set(normed[token_index])  82.9 us
    dot_general x7, matrix products, on_device(): jnp.einsum('nesf,efd->nesd', inner, w_down, preferred_element_type=jnp.fl...  47.4 us
    dot_general x7, matrix products, on_device(): jnp.einsum('nesd,edf->nesf', received, w_gate, preferred_element_type=jnp...  27.6 us
    ppermute x6, waiting for transfers between devices, shifted(): return lax.ppermute(array, axis, pairs)  27 us
    all_to_all x7, starting transfers between devices, on_device(): lax.all_to_all(jnp.einsum('nesf,efd->nesd', inner, w_down, preferred_elem...  24.8 us
    gather x7, local copies, waits for them, and re-layouts, on_device(): picked = returned[flat_ids, slot_index].reshape(tok_rows, topk, width)  17 us
  transfers between devices with their start and end apart: 13, of which 13 were waited for; matrix products, arithmetic and copies ran while one was open for 1% of the time, Pallas kernels for 0%

commit v1 on v0

--- a/solution.py
+++ b/solution.py
@@ -5,6 +5,27 @@
 
 MB = 4
 EPSILON = 1e-06
+
+
+def hold_cards_by_axis(buf, ax_name, dim_no, on_dim):
+    piece_next = lax.axis_size(ax_name)
+    passed = lax.axis_index(ax_name)
+    w_next, side_arr = (piece_next, passed)
+    z_new = list(buf.shape)
+    seen_now = buf.shape[dim_no] // w_next
+    z_new[dim_no] = seen_now
+    arr_out = z_new[on_dim]
+    z_new[on_dim] = arr_out * w_next
+    z2 = jnp.zeros(z_new, buf.dtype)
+    for rr in range(w_next):
+        earlier = lax.dynamic_slice_in_dim(buf, (side_arr ^ rr) * seen_now, seen_now, axis=dim_no)
+        if rr:
+            store = []
+            for p in range(w_next):
+                store.append((p, p ^ rr))
+            earlier = lax.ppermute(earlier, ax_name, store)
+        z2 = lax.dynamic_update_slice_in_dim(z2, earlier, (side_arr ^ rr) * arr_out, axis=on_dim)
+    return z2
 
 
 def shifted(array, axis, by):
@@ -68,14 +89,13 @@
         )
         up_part = jnp.einsum("nesd,edf->nesf", received, w_up, preferred_element_type=jnp.float32)
         inner = (jax.nn.silu(gate_part) * up_part).astype(jnp.bfloat16)
-        returned = lax.all_to_all(
+        returned = hold_cards_by_axis(
             jnp.einsum("nesf,efd->nesd", inner, w_down, preferred_element_type=jnp.float32).astype(
                 jnp.bfloat16
             ),
             "expert",
-            split_axis=0,
-            concat_axis=0,
-            tiled=True,
+            dim_no=0,
+            on_dim=0,
         )
         returned = returned.reshape(experts, capacity, width)
         picked = returned[flat_ids, slot_index].reshape(tok_rows, topk, width)

time: 608 us -> 579 us (0.952)
  blocking collectives: 166 us -> 0 us
  starting transfers between devices: 40.1 us -> 112 us
  waiting for transfers between devices: 168 us -> 231 us
    all_to_all x7 -> x0, blocking collectives: 166 us -> none  [on_device(): lax.all_to_all(outgoing, 'expert', split_axis=0, concat_axis=0, tiled=True)]
    ppermute x0 -> x49, starting transfers between devices: none -> 59.4 us  [hold_cards_by_axis(): earlier = lax.ppermute(earlier, ax_name, store)]
    ppermute x0 -> x49, waiting for transfers between devices: none -> 56.7 us  [hold_cards_by_axis(): earlier = lax.ppermute(earlier, ax_name, store)]
    all_to_all x7, starting transfers between devices: 24.8 us -> 39.1 us  [on_device(): lax.all_to_all(outgoing, 'expert', split_axis=0, concat_axis=0, tiled=True)]
    convert_element_type x7 -> x0, local copies, waits for them, and re-layouts: 11.8 us -> none  [on_device(): jnp.einsum('nesf,efd->nesd', inner, w_down, preferred_element_type=jnp.fl...]
    another operation x7 -> x70, local copies, waits for them, and re-layouts: 0.54 us -> 9.97 us
    reshape x14, local copies, waits for them, and re-layouts: 7.68 us -> 14 us  [on_device(): outgoing = outgoing.reshape(devices, local_experts, capacity, width)]
  transfers between devices with their start and end apart: 13 -> 62, of which waited for: 13 -> 27; matrix products, arithmetic and copies ran while one was open for 1% -> 3% of each run, Pallas kernels for 0% -> 0%
where the time goes in v1:
time: 579 us; the launch traced here: 571 us
  waiting for transfers between devices  231 us (40%)
  local copies, waits for them, and re-layouts  141 us (24%)
  starting transfers between devices  112 us (19%)
  matrix products  75.2 us (13%)
  other arithmetic  10 us (2%)
    all_to_all x7, waiting for transfers between devices, on_device(): lax.all_to_all(outgoing, 'expert', split_axis=0, concat_axis=0, tiled=True)  142 us
    scatter x7, local copies, waits for them, and re-layouts, on_device(): outgoing = outgoing.at[flat_ids, slot_index].set(normed[token_index])  82.9 us
    ppermute x49, starting transfers between devices, hold_cards_by_axis(): earlier = lax.ppermute(earlier, ax_name, store)  59.4 us
    ppermute x49, waiting for transfers between devices, hold_cards_by_axis(): earlier = lax.ppermute(earlier, ax_name, store)  56.7 us
    dot_general x7, matrix products, on_device(): jnp.einsum('nesf,efd->nesd', inner, w_down, preferred_element_type=jnp.fl...  47.5 us
    all_to_all x7, starting transfers between devices, on_device(): lax.all_to_all(outgoing, 'expert', split_axis=0, concat_axis=0, tiled=True)  39.1 us
    ppermute x6, waiting for transfers between devices, shifted(): return lax.ppermute(array, axis, pairs)  32.3 us
    dot_general x7, matrix products, on_device(): jnp.einsum('nesd,edf->nesf', received, w_gate, preferred_element_type=jnp...  27.7 us
  transfers between devices with their start and end apart: 62, of which 27 were waited for; matrix products, arithmetic and copies ran while one was open for 3% of the time, Pallas kernels for 0%

profile of v1, /device:TPU:4, one launch (start us, length us, event | category | flops | bytes accessed | tf_op | source)
XLA Modules:
  0.0 571.4 jit_solution(6535417229599122050)
XLA Ops:
  4.5 11.8 %scatter_fusion = bf16[16,12,2048]{2,0,1:T(8,128)(2,1)S(1)} fusion(bf16[16,12,2048]{2,0,1:T(8,128)(2,1)S(1)} %broadcast.479.clone, s32[128]{0:T(128)S(1)} %get-tuple-element.46, bf16[128,2048]{1,0:T(8,128)(2,1)S(1)} %gather_fusion), kind=kCustom, calls=%fused_computation.14 | custom fusion | bytes 1573888 | tf_op jit(solution)/shard_map/scatter | solution.py:84
  18.4 5.4 all-to-all-start
  25.2 19.6 %all-to-all-done = bf16[8,2,12,2048]{3,1,2,0:T(2,128)(2,1)S(1)} async-done(((bf16[8,2,12,2048]{3,1,2,0:T(2,128)(2,1)}), bf16[8,2,12,2048]{3,1,2,0:T(2,128)(2,1)S(1)}, u32[]{:S(2)}, u32[]{:S(2)}) %all-to-all-start) | async-done | bytes 786464 | tf_op jit(solution)/shard_map/all_to_all | solution.py:86
  44.7 4.0 fusion.63
  48.7 6.8 %fusion.42 = bf16[2,8,12,2048]{3,2,1,0:T(8,128)(2,1)S(1)} fusion(bf16[1,2,768,2048]{3,2,1,0:T(8,128)(2,1)} %param.11, bf16[1,2,2048,768]{3,2,1,0:T(8,128)(2,1)} %param.10, bf16[8,2,12,2048]{3,1,2,0:T(2,128)(2,1)S(1)} %all-to-all-done, f32[8,2,12,768]{3,2,0,1:T(8,128)S(1)} %fusion.63), kind=kOutput, calls=%fused_computation.63 | convolution fusion | flops 1209237504 | bytes 14745600 | tf_op jit(solution)/shard_map/nesf,efd->nesd/dot_general | solution.py:93
  58.4 2.5 collective-permute-start.4
  65.9 7.3 %collective-permute-done.3 = bf16[1,2,12,2048]{3,1,2,0:T(2,128)(2,1)S(1)} collective-permute-done((bf16[1,2,12,2048]{3,1,2,0:T(2,128)(2,1)S(1)}, bf16[1,2,12,2048]{3,1,2,0:T(2,128)(2,1)S(1)}, u32[]{:S(2)}, u32[]{:S(2)}) %collective-permute-start.3) | collective-permute-done | bytes 98336 | tf_op jit(solution)/shard_map/ppermute | solution.py:26
  74.6 2.4 gather_fusion.1
  77.5 3.6 collective-permute-start.7
  81.2 4.0 collective-permute-done.7
  86.5 11.8 %scatter_fusion.1 = bf16[16,12,2048]{2,0,1:T(8,128)(2,1)S(1)} fusion(bf16[16,12,2048]{2,0,1:T(8,128)(2,1)S(1)} %broadcast.479.clone.1, s32[128]{0:T(128)S(1)} %get-tuple-element.44, bf16[128,2048]{1,0:T(8,128)(2,1)S(1)} %gather_fusion.2), kind=kCustom, calls=%fused_computation.15 | custom fusion | bytes 1573888 | tf_op jit(solution)/shard_map/scatter | solution.py:84
  100.3 5.4 all-to-all-start.1
  106.0 20.8 %all-to-all-done.1 = bf16[8,2,12,2048]{3,1,2,0:T(2,128)(2,1)S(1)} async-done(((bf16[8,2,12,2048]{3,1,2,0:T(2,128)(2,1)}), bf16[8,2,12,2048]{3,1,2,0:T(2,128)(2,1)S(1)}, u32[]{:S(2)}, u32[]{:S(2)}) %all-to-all-start.1) | async-done | bytes 786464 | tf_op jit(solution)/shard_map/all_to_all | solution.py:86
  126.7 4.0 fusion.66
  130.7 6.8 %fusion.45 = bf16[2,8,12,2048]{3,2,1,0:T(8,128)(2,1)S(1)} fusion(bf16[1,2,768,2048]{3,2,1,0:T(8,128)(2,1)} %param.11, bf16[1,2,2048,768]{3,2,1,0:T(8,128)(2,1)} %param.10, bf16[8,2,12,2048]{3,1,2,0:T(2,128)(2,1)S(1)} %all-to-all-done.1, f32[8,2,12,768]{3,2,0,1:T(8,128)S(1)} %fusion.66), kind=kOutput, calls=%fused_computation.64 | convolution fusion | flops 1209237504 | bytes 14745600 | tf_op jit(solution)/shard_map/nesf,efd->nesd/dot_general | solution.py:93
  140.3 2.5 collective-permute-start.12
  147.8 7.3 %collective-permute-done.11 = bf16[1,2,12,2048]{3,1,2,0:T(2,128)(2,1)S(1)} collective-permute-done((bf16[1,2,12,2048]{3,1,2,0:T(2,128)(2,1)S(1)}, bf16[1,2,12,2048]{3,1,2,0:T(2,128)(2,1)S(1)}, u32[]{:S(2)}, u32[]{:S(2)}) %collective-permute-start.11) | collective-permute-done | bytes 98336 | tf_op jit(solution)/shard_map/ppermute | solution.py:26
  156.6 2.4 gather_fusion.3
  159.5 2.5 collective-permute-start.15
  162.0 5.2 collective-permute-done.15
  168.5 11.8 %scatter_fusion.2 = bf16[16,12,2048]{2,0,1:T(8,128)(2,1)S(1)} fusion(bf16[16,12,2048]{2,0,1:T(8,128)(2,1)S(1)} %broadcast.479.clone.2, s32[128]{0:T(128)S(1)} %get-tuple-element.38, bf16[128,2048]{1,0:T(8,128)(2,1)S(1)} %gather_fusion.4), kind=kCustom, calls=%fused_computation.16 | custom fusion | bytes 1573888 | tf_op jit(solution)/shard_map/scatter | solution.py:84
  182.4 5.8 %all-to-all-start.2 = ((bf16[8,2,12,2048]{3,1,2,0:T(2,128)(2,1)}), bf16[8,2,12,2048]{3,1,2,0:T(2,128)(2,1)S(1)}, u32[]{:S(2)}, u32[]{:S(2)}) async-start(bf16[8,2,12,2048]{3,1,2,0:T(2,128)(2,1)} %copy.216), calls=%async_computation.2 | async-start | bytes 1572864 | tf_op jit(solution)/shard_map/all_to_all | solution.py:86
  189.4 19.7 %all-to-all-done.2 = bf16[8,2,12,2048]{3,1,2,0:T(2,128)(2,1)S(1)} async-done(((bf16[8,2,12,2048]{3,1,2,0:T(2,128)(2,1)}), bf16[8,2,12,2048]{3,1,2,0:T(2,128)(2,1)S(1)}, u32[]{:S(2)}, u32[]{:S(2)}) %all-to-all-start.2) | async-done | bytes 786464 | tf_op jit(solution)/shard_map/all_to_all | solution.py:86
  209.1 4.0 fusion.69
  213.1 6.8 %fusion.48 = bf16[2,8,12,2048]{3,2,1,0:T(8,128)(2,1)S(1)} fusion(bf16[1,2,768,2048]{3,2,1,0:T(8,128)(2,1)} %param.11, bf16[1,2,2048,768]{3,2,1,0:T(8,128)(2,1)} %param.10, bf16[8,2,12,2048]{3,1,2,0:T(2,128)(2,1)S(1)} %all-to-all-done.2, f32[8,2,12,768]{3,2,0,1:T(8,128)S(1)} %fusion.69), kind=kOutput, calls=%fused_computation.65 | convolution fusion | flops 1209237504 | bytes 14745600 | tf_op jit(solution)/shard_map/nesf,efd->nesd/dot_general | solution.py:93
  222.7 2.5 collective-permute-start.20
  230.2 7.2 %collective-permute-done.19 = bf16[1,2,12,2048]{3,1,2,0:T(2,128)(2,1)S(1)} collective-permute-done((bf16[1,2,12,2048]{3,1,2,0:T(2,128)(2,1)S(1)}, bf16[1,2,12,2048]{3,1,2,0:T(2,128)(2,1)S(1)}, u32[]{:S(2)}, u32[]{:S(2)}) %collective-permute-start.19) | collective-permute-done | bytes 98336 | tf_op jit(solution)/shard_map/ppermute | solution.py:26
  239.0 2.4 gather_fusion.5
  243.8 5.8 %collective-permute-done.23 = bf16[16,2048]{1,0:T(8,128)(2,1)S(1)} collective-permute-done((bf16[16,2048]{1,0:T(8,128)(2,1)S(1)}, bf16[16,2048]{1,0:T(8,128)(2,1)S(1)}, u32[]{:S(2)}, u32[]{:S(2)}) %collective-permute-start.23) | collective-permute-done | bytes 65568 | tf_op jit(solution)/shard_map/ppermute | solution.py:34
  250.9 11.8 %scatter_fusion.3 = bf16[16,12,2048]{2,0,1:T(8,128)(2,1)S(1)} fusion(bf16[16,12,2048]{2,0,1:T(8,128)(2,1)S(1)} %broadcast.479.clone.3, s32[128]{0:T(128)S(1)} %get-tuple-element.32, bf16[128,2048]{1,0:T(8,128)(2,1)S(1)} %gather_fusion.6), kind=kCustom, calls=%fused_computation.17 | custom fusion | bytes 1573888 | tf_op jit(solution)/shard_map/scatter | solution.py:84
  264.7 5.5 all-to-all-start.3
  270.4 20.8 %all-to-all-done.3 = bf16[8,2,12,2048]{3,1,2,0:T(2,128)(2,1)S(1)} async-done(((bf16[8,2,12,2048]{3,1,2,0:T(2,128)(2,1)}), bf16[8,2,12,2048]{3,1,2,0:T(2,128)(2,1)S(1)}, u32[]{:S(2)}, u32[]{:S(2)}) %all-to-all-start.3) | async-done | bytes 786464 | tf_op jit(solution)/shard_map/all_to_all | solution.py:86
  291.2 3.9 fusion.72
  295.2 6.8 %fusion.51 = bf16[2,8,12,2048]{3,2,1,0:T(8,128)(2,1)S(1)} fusion(bf16[1,2,768,2048]{3,2,1,0:T(8,128)(2,1)} %param.11, bf16[1,2,2048,768]{3,2,1,0:T(8,128)(2,1)} %param.10, bf16[8,2,12,2048]{3,1,2,0:T(2,128)(2,1)S(1)} %all-to-all-done.3, f32[8,2,12,768]{3,2,0,1:T(8,128)S(1)} %fusion.72), kind=kOutput, calls=%fused_computation.66 | convolution fusion | flops 1209237504 | bytes 14745600 | tf_op jit(solution)/shard_map/nesf,efd->nesd/dot_general | solution.py:93
  304.8 2.5 collective-permute-start.28
  312.3 7.2 %collective-permute-done.27 = bf16[1,2,12,2048]{3,1,2,0:T(2,128)(2,1)S(1)} collective-permute-done((bf16[1,2,12,2048]{3,1,2,0:T(2,128)(2,1)S(1)}, bf16[1,2,12,2048]{3,1,2,0:T(2,128)(2,1)S(1)}, u32[]{:S(2)}, u32[]{:S(2)}) %collective-permute-start.27) | collective-permute-done | bytes 98336 | tf_op jit(solution)/shard_map/ppermute | solution.py:26
  321.1 2.4 gather_fusion.7
  325.9 5.8 %collective-permute-done.31 = bf16[16,2048]{1,0:T(8,128)(2,1)S(1)} collective-permute-done((bf16[16,2048]{1,0:T(8,128)(2,1)S(1)}, bf16[16,2048]{1,0:T(8,128)(2,1)S(1)}, u32[]{:S(2)}, u32[]{:S(2)}) %collective-permute-start.31) | collective-permute-done | bytes 65568 | tf_op jit(solution)/shard_map/ppermute | solution.py:34
  333.0 11.9 %scatter_fusion.4 = bf16[16,12,2048]{2,0,1:T(8,128)(2,1)S(1)} fusion(bf16[16,12,2048]{2,0,1:T(8,128)(2,1)S(1)} %broadcast.479.clone.4, s32[128]{0:T(128)S(1)} %get-tuple-element.26, bf16[128,2048]{1,0:T(8,128)(2,1)S(1)} %gather_fusion.8), kind=kCustom, calls=%fused_computation.18 | custom fusion | bytes 1573888 | tf_op jit(solution)/shard_map/scatter | solution.py:84
  346.9 5.6 all-to-all-start.4
  353.7 19.7 %all-to-all-done.4 = bf16[8,2,12,2048]{3,1,2,0:T(2,128)(2,1)S(1)} async-done(((bf16[8,2,12,2048]{3,1,2,0:T(2,128)(2,1)}), bf16[8,2,12,2048]{3,1,2,0:T(2,128)(2,1)S(1)}, u32[]{:S(2)}, u32[]{:S(2)}) %all-to-all-start.4) | async-done | bytes 786464 | tf_op jit(solution)/shard_map/all_to_all | solution.py:86
  373.4 4.0 fusion.75
  377.4 6.8 %fusion.54 = bf16[2,8,12,2048]{3,2,1,0:T(8,128)(2,1)S(1)} fusion(bf16[1,2,768,2048]{3,2,1,0:T(8,128)(2,1)} %param.11, bf16[1,2,2048,768]{3,2,1,0:T(8,128)(2,1)} %param.10, bf16[8,2,12,2048]{3,1,2,0:T(2,128)(2,1)S(1)} %all-to-all-done.4, f32[8,2,12,768]{3,2,0,1:T(8,128)S(1)} %fusion.75), kind=kOutput, calls=%fused_computation.67 | convolution fusion | flops 1209237504 | bytes 14745600 | tf_op jit(solution)/shard_map/nesf,efd->nesd/dot_general | solution.py:93
  387.0 2.5 collective-permute-start.36
  394.5 7.3 %collective-permute-done.35 = bf16[1,2,12,2048]{3,1,2,0:T(2,128)(2,1)S(1)} collective-permute-done((bf16[1,2,12,2048]{3,1,2,0:T(2,128)(2,1)S(1)}, bf16[1,2,12,2048]{3,1,2,0:T(2,128)(2,1)S(1)}, u32[]{:S(2)}, u32[]{:S(2)}) %collective-permute-start.35) | collective-permute-done | bytes 98336 | tf_op jit(solution)/shard_map/ppermute | solution.py:26
  403.2 2.4 gather_fusion.9
  408.1 5.8 %collective-permute-done.39 = bf16[16,2048]{1,0:T(8,128)(2,1)S(1)} collective-permute-done((bf16[16,2048]{1,0:T(8,128)(2,1)S(1)}, bf16[16,2048]{1,0:T(8,128)(2,1)S(1)}, u32[]{:S(2)}, u32[]{:S(2)}) %collective-permute-start.39) | collective-permute-done | bytes 65568 | tf_op jit(solution)/shard_map/ppermute | solution.py:34
  415.1 11.8 %scatter_fusion.5 = bf16[16,12,2048]{2,0,1:T(8,128)(2,1)S(1)} fusion(bf16[16,12,2048]{2,0,1:T(8,128)(2,1)S(1)} %broadcast.479.clone.5, s32[128]{0:T(128)S(1)} %get-tuple-element.20, bf16[128,2048]{1,0:T(8,128)(2,1)S(1)} %gather_fusion.10), kind=kCustom, calls=%fused_computation.19 | custom fusion | bytes 1573888 | tf_op jit(solution)/shard_map/scatter | solution.py:84
  429.0 5.8 %all-to-all-start.5 = ((bf16[8,2,12,2048]{3,1,2,0:T(2,128)(2,1)}), bf16[8,2,12,2048]{3,1,2,0:T(2,128)(2,1)S(1)}, u32[]{:S(2)}, u32[]{:S(2)}) async-start(bf16[8,2,12,2048]{3,1,2,0:T(2,128)(2,1)} %copy.282), calls=%async_computation.5 | async-start | bytes 1572864 | tf_op jit(solution)/shard_map/all_to_all | solution.py:86
  434.9 20.8 %all-to-all-done.5 = bf16[8,2,12,2048]{3,1,2,0:T(2,128)(2,1)S(1)} async-done(((bf16[8,2,12,2048]{3,1,2,0:T(2,128)(2,1)}), bf16[8,2,12,2048]{3,1,2,0:T(2,128)(2,1)S(1)}, u32[]{:S(2)}, u32[]{:S(2)}) %all-to-all-start.5) | async-done | bytes 786464 | tf_op jit(solution)/shard_map/all_to_all | solution.py:86
  455.7 3.9 fusion.78
  459.7 6.8 %fusion.57 = bf16[2,8,12,2048]{3,2,1,0:T(8,128)(2,1)S(1)} fusion(bf16[1,2,768,2048]{3,2,1,0:T(8,128)(2,1)} %param.11, bf16[1,2,2048,768]{3,2,1,0:T(8,128)(2,1)} %param.10, bf16[8,2,12,2048]{3,1,2,0:T(2,128)(2,1)S(1)} %all-to-all-done.5, f32[8,2,12,768]{3,2,0,1:T(8,128)S(1)} %fusion.78), kind=kOutput, calls=%fused_computation.68 | convolution fusion | flops 1209237504 | bytes 14745600 | tf_op jit(solution)/shard_map/nesf,efd->nesd/dot_general | solution.py:93
  469.3 2.5 collective-permute-start.44
  476.8 7.2 %collective-permute-done.43 = bf16[1,2,12,2048]{3,1,2,0:T(2,128)(2,1)S(1)} collective-permute-done((bf16[1,2,12,2048]{3,1,2,0:T(2,128)(2,1)S(1)}, bf16[1,2,12,2048]{3,1,2,0:T(2,128)(2,1)S(1)}, u32[]{:S(2)}, u32[]{:S(2)}) %collective-permute-start.43) | collective-permute-done | bytes 98336 | tf_op jit(solution)/shard_map/ppermute | solution.py:26
  485.6 2.4 gather_fusion.11
  490.4 5.8 %collective-permute-done.47 = bf16[16,2048]{1,0:T(8,128)(2,1)S(1)} collective-permute-done((bf16[16,2048]{1,0:T(8,128)(2,1)S(1)}, bf16[16,2048]{1,0:T(8,128)(2,1)S(1)}, u32[]{:S(2)}, u32[]{:S(2)}) %collective-permute-start.47) | collective-permute-done | bytes 65568 | tf_op jit(solution)/shard_map/ppermute | solution.py:34
  497.5 11.8 %scatter_fusion.6 = bf16[16,12,2048]{2,0,1:T(8,128)(2,1)S(1)} fusion(bf16[16,12,2048]{2,0,1:T(8,128)(2,1)S(1)} %broadcast.479, s32[128]{0:T(128)S(1)} %get-tuple-element.14, bf16[128,2048]{1,0:T(8,128)(2,1)S(1)} %gather_fusion.12), kind=kCustom, calls=%fused_computation.20 | custom fusion | bytes 1573888 | tf_op jit(solution)/shard_map/scatter | solution.py:84
  511.3 5.6 all-to-all-start.6
  517.7 20.2 %all-to-all-done.6 = bf16[8,2,12,2048]{3,1,2,0:T(2,128)(2,1)S(1)} async-done(((bf16[8,2,12,2048]{3,1,2,0:T(2,128)(2,1)}), bf16[8,2,12,2048]{3,1,2,0:T(2,128)(2,1)S(1)}, u32[]{:S(2)}, u32[]{:S(2)}) %all-to-all-start.6) | async-done | bytes 786464 | tf_op jit(solution)/shard_map/all_to_all | solution.py:86
  537.8 3.9 fusion.81
  541.8 6.8 %fusion.60 = bf16[2,8,12,2048]{3,2,1,0:T(8,128)(2,1)S(1)} fusion(bf16[1,2,768,2048]{3,2,1,0:T(8,128)(2,1)} %param.11, bf16[1,2,2048,768]{3,2,1,0:T(8,128)(2,1)} %param.10, bf16[8,2,12,2048]{3,1,2,0:T(2,128)(2,1)S(1)} %all-to-all-done.6, f32[8,2,12,768]{3,2,0,1:T(8,128)S(1)} %fusion.81), kind=kOutput, calls=%fused_computation.69 | convolution fusion | flops 1209237504 | bytes 14745600 | tf_op jit(solution)/shard_map/nesf,efd->nesd/dot_general | solution.py:93
  551.4 2.5 collective-permute-start.52
  556.3 2.4 collective-permute-start.54
  558.9 7.2 %collective-permute-done.51 = bf16[1,2,12,2048]{3,1,2,0:T(2,128)(2,1)S(1)} collective-permute-done((bf16[1,2,12,2048]{3,1,2,0:T(2,128)(2,1)S(1)}, bf16[1,2,12,2048]{3,1,2,0:T(2,128)(2,1)S(1)}, u32[]{:S(2)}, u32[]{:S(2)}) %collective-permute-start.51) | collective-permute-done | bytes 98336 | tf_op jit(solution)/shard_map/ppermute | solution.py:26
  (344 shorter events, 106.5 us)
Async XLA Ops:
  18.4 26.4 %all-to-all-start = ((bf16[8,2,12,2048]{3,1,2,0:T(2,128)(2,1)}), bf16[8,2,12,2048]{3,1,2,0:T(2,128)(2,1)S(1)}, u32[]{:S(2)}, u32[]{:S(2)}) async-start(bf16[8,2,12,2048]{3,1,2,0:T(2,128)(2,1)} %copy.172), calls=%async_computation | async-start | bytes 1572864 | tf_op jit(solution)/shard_map/all_to_all | solution.py:86
  55.5 22.0 %copy-start = (bf16[4,16,2048]{2,1,0:T(8,128)(2,1)S(1)}, bf16[4,16,2048]{2,1,0:T(8,128)(2,1)}, u32[]{:S(2)}) copy-start(bf16[4,16,2048]{2,1,0:T(8,128)(2,1)} %param.7) | copy-start | bytes 786436
  55.5 29.8 %copy-start.1 = (f32[1,2048]{1,0:T(1,128)S(1)}, f32[1,2048]{1,0:T(1,128)}, u32[]{:S(2)}) copy-start(f32[1,2048]{1,0:T(1,128)} %param.8) | copy-start | bytes 24580
  55.8 6.0 %collective-permute-start = (bf16[1,2,12,2048]{3,1,2,0:T(2,128)(2,1)S(1)}, bf16[1,2,12,2048]{3,1,2,0:T(2,128)(2,1)S(1)}, u32[]{:S(2)}, u32[]{:S(2)}) collective-permute-start(bf16[1,2,12,2048]{3,1,2,0:T(2,128)(2,1)S(1)} %bitcast.754), channel_id=1, source_target_pairs={{0,1},{1,0},{2,3},{3,2},{4,5},{5,4},{6,7},{7,6},{8,9},{9,8},{10,11... | collective-permute-start | bytes 294920 | tf_op jit(solution)/shard_map/ppermute | solution.py:26
  55.9 7.3 %collective-permute-start.1 = (bf16[1,2,12,2048]{3,1,2,0:T(2,128)(2,1)S(1)}, bf16[1,2,12,2048]{3,1,2,0:T(2,128)(2,1)S(1)}, u32[]{:S(2)}, u32[]{:S(2)}) collective-permute-start(bf16[1,2,12,2048]{3,1,2,0:T(2,128)(2,1)S(1)} %bitcast.747), channel_id=1, source_target_pairs={{0,2},{1,3},{2,0},{3,1},{4,6},{5,7},{6,4},{7,5},{8,10},{9,11},{10,... | collective-permute-start | bytes 294920 | tf_op jit(solution)/shard_map/ppermute | solution.py:26
  56.1 9.6 %collective-permute-start.2 = (bf16[1,2,12,2048]{3,1,2,0:T(2,128)(2,1)S(1)}, bf16[1,2,12,2048]{3,1,2,0:T(2,128)(2,1)S(1)}, u32[]{:S(2)}, u32[]{:S(2)}) collective-permute-start(bf16[1,2,12,2048]{3,1,2,0:T(2,128)(2,1)S(1)} %bitcast.734), channel_id=1, source_target_pairs={{0,3},{1,2},{2,1},{3,0},{4,7},{5,6},{6,5},{7,4},{8,11},{9,10},{10,... | collective-permute-start | bytes 294920 | tf_op jit(solution)/shard_map/ppermute | solution.py:26
  58.1 15.0 %collective-permute-start.3 = (bf16[1,2,12,2048]{3,1,2,0:T(2,128)(2,1)S(1)}, bf16[1,2,12,2048]{3,1,2,0:T(2,128)(2,1)S(1)}, u32[]{:S(2)}, u32[]{:S(2)}) collective-permute-start(bf16[1,2,12,2048]{3,1,2,0:T(2,128)(2,1)S(1)} %bitcast.728), channel_id=1, source_target_pairs={{0,4},{1,5},{2,6},{3,7},{4,0},{5,1},{6,2},{7,3},{8,12},{9,13},{10,... | collective-permute-start | bytes 294920 | tf_op jit(solution)/shard_map/ppermute | solution.py:26
  58.4 15.6 %collective-permute-start.4 = (bf16[1,2,12,2048]{3,1,2,0:T(2,128)(2,1)S(1)}, bf16[1,2,12,2048]{3,1,2,0:T(2,128)(2,1)S(1)}, u32[]{:S(2)}, u32[]{:S(2)}) collective-permute-start(bf16[1,2,12,2048]{3,1,2,0:T(2,128)(2,1)S(1)} %bitcast.722), channel_id=1, source_target_pairs={{0,5},{1,4},{2,7},{3,6},{4,1},{5,0},{6,3},{7,2},{8,13},{9,12},{10,... | collective-permute-start | bytes 294920 | tf_op jit(solution)/shard_map/ppermute | solution.py:26
  61.8 12.3 %collective-permute-start.5 = (bf16[1,2,12,2048]{3,1,2,0:T(2,128)(2,1)S(1)}, bf16[1,2,12,2048]{3,1,2,0:T(2,128)(2,1)S(1)}, u32[]{:S(2)}, u32[]{:S(2)}) collective-permute-start(bf16[1,2,12,2048]{3,1,2,0:T(2,128)(2,1)S(1)} %bitcast.740), channel_id=1, source_target_pairs={{0,6},{1,7},{2,4},{3,5},{4,2},{5,3},{6,0},{7,1},{8,14},{9,15},{10,... | collective-permute-start | bytes 294920 | tf_op jit(solution)/shard_map/ppermute | solution.py:26
  63.3 10.9 %collective-permute-start.6 = (bf16[1,2,12,2048]{3,1,2,0:T(2,128)(2,1)S(1)}, bf16[1,2,12,2048]{3,1,2,0:T(2,128)(2,1)S(1)}, u32[]{:S(2)}, u32[]{:S(2)}) collective-permute-start(bf16[1,2,12,2048]{3,1,2,0:T(2,128)(2,1)S(1)} %bitcast.716), channel_id=1, source_target_pairs={{0,7},{1,6},{2,5},{3,4},{4,3},{5,2},{6,1},{7,0},{8,15},{9,14},{10,... | collective-permute-start | bytes 294920 | tf_op jit(solution)/shard_map/ppermute | solution.py:26
  77.5 7.7 %collective-permute-start.7 = (bf16[16,2048]{1,0:T(8,128)(2,1)S(1)}, bf16[16,2048]{1,0:T(8,128)(2,1)S(1)}, u32[]{:S(2)}, u32[]{:S(2)}) collective-permute-start(bf16[16,2048]{1,0:T(8,128)(2,1)S(1)} %fusion.267), channel_id=1, source_target_pairs={{0,8},{8,16},{16,24},{1,9},{9,17},{17,25},{2,10},{10,18},{18,26},{... | collective-permute-start | bytes 196616 | tf_op jit(solution)/shard_map/ppermute | solution.py:34
  100.3 26.4 %all-to-all-start.1 = ((bf16[8,2,12,2048]{3,1,2,0:T(2,128)(2,1)}), bf16[8,2,12,2048]{3,1,2,0:T(2,128)(2,1)S(1)}, u32[]{:S(2)}, u32[]{:S(2)}) async-start(bf16[8,2,12,2048]{3,1,2,0:T(2,128)(2,1)} %copy.194), calls=%async_computation.1 | async-start | bytes 1572864 | tf_op jit(solution)/shard_map/all_to_all | solution.py:86
  137.7 6.0 %collective-permute-start.8 = (bf16[1,2,12,2048]{3,1,2,0:T(2,128)(2,1)S(1)}, bf16[1,2,12,2048]{3,1,2,0:T(2,128)(2,1)S(1)}, u32[]{:S(2)}, u32[]{:S(2)}) collective-permute-start(bf16[1,2,12,2048]{3,1,2,0:T(2,128)(2,1)S(1)} %bitcast.755), channel_id=1, source_target_pairs={{0,1},{1,0},{2,3},{3,2},{4,5},{5,4},{6,7},{7,6},{8,9},{9,8},{10,11... | collective-permute-start | bytes 294920 | tf_op jit(solution)/shard_map/ppermute | solution.py:26
  137.9 7.3 %collective-permute-start.9 = (bf16[1,2,12,2048]{3,1,2,0:T(2,128)(2,1)S(1)}, bf16[1,2,12,2048]{3,1,2,0:T(2,128)(2,1)S(1)}, u32[]{:S(2)}, u32[]{:S(2)}) collective-permute-start(bf16[1,2,12,2048]{3,1,2,0:T(2,128)(2,1)S(1)} %bitcast.748), channel_id=1, source_target_pairs={{0,2},{1,3},{2,0},{3,1},{4,6},{5,7},{6,4},{7,5},{8,10},{9,11},{10,... | collective-permute-start | bytes 294920 | tf_op jit(solution)/shard_map/ppermute | solution.py:26
  138.1 9.6 %collective-permute-start.10 = (bf16[1,2,12,2048]{3,1,2,0:T(2,128)(2,1)S(1)}, bf16[1,2,12,2048]{3,1,2,0:T(2,128)(2,1)S(1)}, u32[]{:S(2)}, u32[]{:S(2)}) collective-permute-start(bf16[1,2,12,2048]{3,1,2,0:T(2,128)(2,1)S(1)} %bitcast.735), channel_id=1, source_target_pairs={{0,3},{1,2},{2,1},{3,0},{4,7},{5,6},{6,5},{7,4},{8,11},{9,10},{10,... | collective-permute-start | bytes 294920 | tf_op jit(solution)/shard_map/ppermute | solution.py:26
  140.1 15.0 %collective-permute-start.11 = (bf16[1,2,12,2048]{3,1,2,0:T(2,128)(2,1)S(1)}, bf16[1,2,12,2048]{3,1,2,0:T(2,128)(2,1)S(1)}, u32[]{:S(2)}, u32[]{:S(2)}) collective-permute-start(bf16[1,2,12,2048]{3,1,2,0:T(2,128)(2,1)S(1)} %bitcast.729), channel_id=1, source_target_pairs={{0,4},{1,5},{2,6},{3,7},{4,0},{5,1},{6,2},{7,3},{8,12},{9,13},{10,... | collective-permute-start | bytes 294920 | tf_op jit(solution)/shard_map/ppermute | solution.py:26
  140.3 15.6 %collective-permute-start.12 = (bf16[1,2,12,2048]{3,1,2,0:T(2,128)(2,1)S(1)}, bf16[1,2,12,2048]{3,1,2,0:T(2,128)(2,1)S(1)}, u32[]{:S(2)}, u32[]{:S(2)}) collective-permute-start(bf16[1,2,12,2048]{3,1,2,0:T(2,128)(2,1)S(1)} %bitcast.723), channel_id=1, source_target_pairs={{0,5},{1,4},{2,7},{3,6},{4,1},{5,0},{6,3},{7,2},{8,13},{9,12},{10,... | collective-permute-start | bytes 294920 | tf_op jit(solution)/shard_map/ppermute | solution.py:26
  143.8 12.3 %collective-permute-start.13 = (bf16[1,2,12,2048]{3,1,2,0:T(2,128)(2,1)S(1)}, bf16[1,2,12,2048]{3,1,2,0:T(2,128)(2,1)S(1)}, u32[]{:S(2)}, u32[]{:S(2)}) collective-permute-start(bf16[1,2,12,2048]{3,1,2,0:T(2,128)(2,1)S(1)} %bitcast.741), channel_id=1, source_target_pairs={{0,6},{1,7},{2,4},{3,5},{4,2},{5,3},{6,0},{7,1},{8,14},{9,15},{10,... | collective-permute-start | bytes 294920 | tf_op jit(solution)/shard_map/ppermute | solution.py:26
  145.2 11.0 %collective-permute-start.14 = (bf16[1,2,12,2048]{3,1,2,0:T(2,128)(2,1)S(1)}, bf16[1,2,12,2048]{3,1,2,0:T(2,128)(2,1)S(1)}, u32[]{:S(2)}, u32[]{:S(2)}) collective-permute-start(bf16[1,2,12,2048]{3,1,2,0:T(2,128)(2,1)S(1)} %bitcast.717), channel_id=1, source_target_pairs={{0,7},{1,6},{2,5},{3,4},{4,3},{5,2},{6,1},{7,0},{8,15},{9,14},{10,... | collective-permute-start | bytes 294920 | tf_op jit(solution)/shard_map/ppermute | solution.py:26
  159.5 7.7 %collective-permute-start.15 = (bf16[16,2048]{1,0:T(8,128)(2,1)S(1)}, bf16[16,2048]{1,0:T(8,128)(2,1)S(1)}, u32[]{:S(2)}, u32[]{:S(2)}) collective-permute-start(bf16[16,2048]{1,0:T(8,128)(2,1)S(1)} %get-tuple-element.41), channel_id=1, source_target_pairs={{0,8},{8,16},{16,24},{1,9},{9,17},{17,25},{2,10},{10,18},{18,26},{... | collective-permute-start | bytes 196616 | tf_op jit(solution)/shard_map/ppermute | solution.py:34
  182.4 26.7 %all-to-all-start.2 = ((bf16[8,2,12,2048]{3,1,2,0:T(2,128)(2,1)}), bf16[8,2,12,2048]{3,1,2,0:T(2,128)(2,1)S(1)}, u32[]{:S(2)}, u32[]{:S(2)}) async-start(bf16[8,2,12,2048]{3,1,2,0:T(2,128)(2,1)} %copy.216), calls=%async_computation.2 | async-start | bytes 1572864 | tf_op jit(solution)/shard_map/all_to_all | solution.py:86
  220.1 6.0 %collective-permute-start.16 = (bf16[1,2,12,2048]{3,1,2,0:T(2,128)(2,1)S(1)}, bf16[1,2,12,2048]{3,1,2,0:T(2,128)(2,1)S(1)}, u32[]{:S(2)}, u32[]{:S(2)}) collective-permute-start(bf16[1,2,12,2048]{3,1,2,0:T(2,128)(2,1)S(1)} %bitcast.756), channel_id=1, source_target_pairs={{0,1},{1,0},{2,3},{3,2},{4,5},{5,4},{6,7},{7,6},{8,9},{9,8},{10,11... | collective-permute-start | bytes 294920 | tf_op jit(solution)/shard_map/ppermute | solution.py:26
  220.3 7.3 %collective-permute-start.17 = (bf16[1,2,12,2048]{3,1,2,0:T(2,128)(2,1)S(1)}, bf16[1,2,12,2048]{3,1,2,0:T(2,128)(2,1)S(1)}, u32[]{:S(2)}, u32[]{:S(2)}) collective-permute-start(bf16[1,2,12,2048]{3,1,2,0:T(2,128)(2,1)S(1)} %bitcast.749), channel_id=1, source_target_pairs={{0,2},{1,3},{2,0},{3,1},{4,6},{5,7},{6,4},{7,5},{8,10},{9,11},{10,... | collective-permute-start | bytes 294920 | tf_op jit(solution)/shard_map/ppermute | solution.py:26
  220.5 9.6 %collective-permute-start.18 = (bf16[1,2,12,2048]{3,1,2,0:T(2,128)(2,1)S(1)}, bf16[1,2,12,2048]{3,1,2,0:T(2,128)(2,1)S(1)}, u32[]{:S(2)}, u32[]{:S(2)}) collective-permute-start(bf16[1,2,12,2048]{3,1,2,0:T(2,128)(2,1)S(1)} %bitcast.736), channel_id=1, source_target_pairs={{0,3},{1,2},{2,1},{3,0},{4,7},{5,6},{6,5},{7,4},{8,11},{9,10},{10,... | collective-permute-start | bytes 294920 | tf_op jit(solution)/shard_map/ppermute | solution.py:26
  222.5 15.0 %collective-permute-start.19 = (bf16[1,2,12,2048]{3,1,2,0:T(2,128)(2,1)S(1)}, bf16[1,2,12,2048]{3,1,2,0:T(2,128)(2,1)S(1)}, u32[]{:S(2)}, u32[]{:S(2)}) collective-permute-start(bf16[1,2,12,2048]{3,1,2,0:T(2,128)(2,1)S(1)} %bitcast.730), channel_id=1, source_target_pairs={{0,4},{1,5},{2,6},{3,7},{4,0},{5,1},{6,2},{7,3},{8,12},{9,13},{10,... | collective-permute-start | bytes 294920 | tf_op jit(solution)/shard_map/ppermute | solution.py:26
  222.7 15.6 %collective-permute-start.20 = (bf16[1,2,12,2048]{3,1,2,0:T(2,128)(2,1)S(1)}, bf16[1,2,12,2048]{3,1,2,0:T(2,128)(2,1)S(1)}, u32[]{:S(2)}, u32[]{:S(2)}) collective-permute-start(bf16[1,2,12,2048]{3,1,2,0:T(2,128)(2,1)S(1)} %bitcast.724), channel_id=1, source_target_pairs={{0,5},{1,4},{2,7},{3,6},{4,1},{5,0},{6,3},{7,2},{8,13},{9,12},{10,... | collective-permute-start | bytes 294920 | tf_op jit(solution)/shard_map/ppermute | solution.py:26
  226.2 12.3 %collective-permute-start.21 = (bf16[1,2,12,2048]{3,1,2,0:T(2,128)(2,1)S(1)}, bf16[1,2,12,2048]{3,1,2,0:T(2,128)(2,1)S(1)}, u32[]{:S(2)}, u32[]{:S(2)}) collective-permute-start(bf16[1,2,12,2048]{3,1,2,0:T(2,128)(2,1)S(1)} %bitcast.742), channel_id=1, source_target_pairs={{0,6},{1,7},{2,4},{3,5},{4,2},{5,3},{6,0},{7,1},{8,14},{9,15},{10,... | collective-permute-start | bytes 294920 | tf_op jit(solution)/shard_map/ppermute | solution.py:26
  227.6 11.0 %collective-permute-start.22 = (bf16[1,2,12,2048]{3,1,2,0:T(2,128)(2,1)S(1)}, bf16[1,2,12,2048]{3,1,2,0:T(2,128)(2,1)S(1)}, u32[]{:S(2)}, u32[]{:S(2)}) collective-permute-start(bf16[1,2,12,2048]{3,1,2,0:T(2,128)(2,1)S(1)} %bitcast.718), channel_id=1, source_target_pairs={{0,7},{1,6},{2,5},{3,4},{4,3},{5,2},{6,1},{7,0},{8,15},{9,14},{10,... | collective-permute-start | bytes 294920 | tf_op jit(solution)/shard_map/ppermute | solution.py:26
  241.9 7.7 %collective-permute-start.23 = (bf16[16,2048]{1,0:T(8,128)(2,1)S(1)}, bf16[16,2048]{1,0:T(8,128)(2,1)S(1)}, u32[]{:S(2)}, u32[]{:S(2)}) collective-permute-start(bf16[16,2048]{1,0:T(8,128)(2,1)S(1)} %get-tuple-element.35), channel_id=1, source_target_pairs={{0,8},{8,16},{16,24},{1,9},{9,17},{17,25},{2,10},{10,18},{18,26},{... | collective-permute-start | bytes 196616 | tf_op jit(solution)/shard_map/ppermute | solution.py:34
  264.7 26.5 %all-to-all-start.3 = ((bf16[8,2,12,2048]{3,1,2,0:T(2,128)(2,1)}), bf16[8,2,12,2048]{3,1,2,0:T(2,128)(2,1)S(1)}, u32[]{:S(2)}, u32[]{:S(2)}) async-start(bf16[8,2,12,2048]{3,1,2,0:T(2,128)(2,1)} %copy.238), calls=%async_computation.3 | async-start | bytes 1572864 | tf_op jit(solution)/shard_map/all_to_all | solution.py:86
  302.2 6.0 %collective-permute-start.24 = (bf16[1,2,12,2048]{3,1,2,0:T(2,128)(2,1)S(1)}, bf16[1,2,12,2048]{3,1,2,0:T(2,128)(2,1)S(1)}, u32[]{:S(2)}, u32[]{:S(2)}) collective-permute-start(bf16[1,2,12,2048]{3,1,2,0:T(2,128)(2,1)S(1)} %bitcast.757), channel_id=1, source_target_pairs={{0,1},{1,0},{2,3},{3,2},{4,5},{5,4},{6,7},{7,6},{8,9},{9,8},{10,11... | collective-permute-start | bytes 294920 | tf_op jit(solution)/shard_map/ppermute | solution.py:26
  302.4 7.3 %collective-permute-start.25 = (bf16[1,2,12,2048]{3,1,2,0:T(2,128)(2,1)S(1)}, bf16[1,2,12,2048]{3,1,2,0:T(2,128)(2,1)S(1)}, u32[]{:S(2)}, u32[]{:S(2)}) collective-permute-start(bf16[1,2,12,2048]{3,1,2,0:T(2,128)(2,1)S(1)} %bitcast.750), channel_id=1, source_target_pairs={{0,2},{1,3},{2,0},{3,1},{4,6},{5,7},{6,4},{7,5},{8,10},{9,11},{10,... | collective-permute-start | bytes 294920 | tf_op jit(solution)/shard_map/ppermute | solution.py:26
  302.6 9.6 %collective-permute-start.26 = (bf16[1,2,12,2048]{3,1,2,0:T(2,128)(2,1)S(1)}, bf16[1,2,12,2048]{3,1,2,0:T(2,128)(2,1)S(1)}, u32[]{:S(2)}, u32[]{:S(2)}) collective-permute-start(bf16[1,2,12,2048]{3,1,2,0:T(2,128)(2,1)S(1)} %bitcast.737), channel_id=1, source_target_pairs={{0,3},{1,2},{2,1},{3,0},{4,7},{5,6},{6,5},{7,4},{8,11},{9,10},{10,... | collective-permute-start | bytes 294920 | tf_op jit(solution)/shard_map/ppermute | solution.py:26
  304.6 15.0 %collective-permute-start.27 = (bf16[1,2,12,2048]{3,1,2,0:T(2,128)(2,1)S(1)}, bf16[1,2,12,2048]{3,1,2,0:T(2,128)(2,1)S(1)}, u32[]{:S(2)}, u32[]{:S(2)}) collective-permute-start(bf16[1,2,12,2048]{3,1,2,0:T(2,128)(2,1)S(1)} %bitcast.731), channel_id=1, source_target_pairs={{0,4},{1,5},{2,6},{3,7},{4,0},{5,1},{6,2},{7,3},{8,12},{9,13},{10,... | collective-permute-start | bytes 294920 | tf_op jit(solution)/shard_map/ppermute | solution.py:26
  304.8 15.6 %collective-permute-start.28 = (bf16[1,2,12,2048]{3,1,2,0:T(2,128)(2,1)S(1)}, bf16[1,2,12,2048]{3,1,2,0:T(2,128)(2,1)S(1)}, u32[]{:S(2)}, u32[]{:S(2)}) collective-permute-start(bf16[1,2,12,2048]{3,1,2,0:T(2,128)(2,1)S(1)} %bitcast.725), channel_id=1, source_target_pairs={{0,5},{1,4},{2,7},{3,6},{4,1},{5,0},{6,3},{7,2},{8,13},{9,12},{10,... | collective-permute-start | bytes 294920 | tf_op jit(solution)/shard_map/ppermute | solution.py:26
  308.2 12.3 %collective-permute-start.29 = (bf16[1,2,12,2048]{3,1,2,0:T(2,128)(2,1)S(1)}, bf16[1,2,12,2048]{3,1,2,0:T(2,128)(2,1)S(1)}, u32[]{:S(2)}, u32[]{:S(2)}) collective-permute-start(bf16[1,2,12,2048]{3,1,2,0:T(2,128)(2,1)S(1)} %bitcast.743), channel_id=1, source_target_pairs={{0,6},{1,7},{2,4},{3,5},{4,2},{5,3},{6,0},{7,1},{8,14},{9,15},{10,... | collective-permute-start | bytes 294920 | tf_op jit(solution)/shard_map/ppermute | solution.py:26
  309.7 11.0 %collective-permute-start.30 = (bf16[1,2,12,2048]{3,1,2,0:T(2,128)(2,1)S(1)}, bf16[1,2,12,2048]{3,1,2,0:T(2,128)(2,1)S(1)}, u32[]{:S(2)}, u32[]{:S(2)}) collective-permute-start(bf16[1,2,12,2048]{3,1,2,0:T(2,128)(2,1)S(1)} %bitcast.719), channel_id=1, source_target_pairs={{0,7},{1,6},{2,5},{3,4},{4,3},{5,2},{6,1},{7,0},{8,15},{9,14},{10,... | collective-permute-start | bytes 294920 | tf_op jit(solution)/shard_map/ppermute | solution.py:26
  324.0 7.7 %collective-permute-start.31 = (bf16[16,2048]{1,0:T(8,128)(2,1)S(1)}, bf16[16,2048]{1,0:T(8,128)(2,1)S(1)}, u32[]{:S(2)}, u32[]{:S(2)}) collective-permute-start(bf16[16,2048]{1,0:T(8,128)(2,1)S(1)} %get-tuple-element.29), channel_id=1, source_target_pairs={{0,8},{8,16},{16,24},{1,9},{9,17},{17,25},{2,10},{10,18},{18,26},{... | collective-permute-start | bytes 196616 | tf_op jit(solution)/shard_map/ppermute | solution.py:34
  346.9 26.5 %all-to-all-start.4 = ((bf16[8,2,12,2048]{3,1,2,0:T(2,128)(2,1)}), bf16[8,2,12,2048]{3,1,2,0:T(2,128)(2,1)S(1)}, u32[]{:S(2)}, u32[]{:S(2)}) async-start(bf16[8,2,12,2048]{3,1,2,0:T(2,128)(2,1)} %copy.260), calls=%async_computation.4 | async-start | bytes 1572864 | tf_op jit(solution)/shard_map/all_to_all | solution.py:86
  384.4 6.0 %collective-permute-start.32 = (bf16[1,2,12,2048]{3,1,2,0:T(2,128)(2,1)S(1)}, bf16[1,2,12,2048]{3,1,2,0:T(2,128)(2,1)S(1)}, u32[]{:S(2)}, u32[]{:S(2)}) collective-permute-start(bf16[1,2,12,2048]{3,1,2,0:T(2,128)(2,1)S(1)} %bitcast.758), channel_id=1, source_target_pairs={{0,1},{1,0},{2,3},{3,2},{4,5},{5,4},{6,7},{7,6},{8,9},{9,8},{10,11... | collective-permute-start | bytes 294920 | tf_op jit(solution)/shard_map/ppermute | solution.py:26
  384.6 7.3 %collective-permute-start.33 = (bf16[1,2,12,2048]{3,1,2,0:T(2,128)(2,1)S(1)}, bf16[1,2,12,2048]{3,1,2,0:T(2,128)(2,1)S(1)}, u32[]{:S(2)}, u32[]{:S(2)}) collective-permute-start(bf16[1,2,12,2048]{3,1,2,0:T(2,128)(2,1)S(1)} %bitcast.751), channel_id=1, source_target_pairs={{0,2},{1,3},{2,0},{3,1},{4,6},{5,7},{6,4},{7,5},{8,10},{9,11},{10,... | collective-permute-start | bytes 294920 | tf_op jit(solution)/shard_map/ppermute | solution.py:26
  384.8 9.6 %collective-permute-start.34 = (bf16[1,2,12,2048]{3,1,2,0:T(2,128)(2,1)S(1)}, bf16[1,2,12,2048]{3,1,2,0:T(2,128)(2,1)S(1)}, u32[]{:S(2)}, u32[]{:S(2)}) collective-permute-start(bf16[1,2,12,2048]{3,1,2,0:T(2,128)(2,1)S(1)} %bitcast.738), channel_id=1, source_target_pairs={{0,3},{1,2},{2,1},{3,0},{4,7},{5,6},{6,5},{7,4},{8,11},{9,10},{10,... | collective-permute-start | bytes 294920 | tf_op jit(solution)/shard_map/ppermute | solution.py:26
  386.7 15.0 %collective-permute-start.35 = (bf16[1,2,12,2048]{3,1,2,0:T(2,128)(2,1)S(1)}, bf16[1,2,12,2048]{3,1,2,0:T(2,128)(2,1)S(1)}, u32[]{:S(2)}, u32[]{:S(2)}) collective-permute-start(bf16[1,2,12,2048]{3,1,2,0:T(2,128)(2,1)S(1)} %bitcast.732), channel_id=1, source_target_pairs={{0,4},{1,5},{2,6},{3,7},{4,0},{5,1},{6,2},{7,3},{8,12},{9,13},{10,... | collective-permute-start | bytes 294920 | tf_op jit(solution)/shard_map/ppermute | solution.py:26
  387.0 15.6 %collective-permute-start.36 = (bf16[1,2,12,2048]{3,1,2,0:T(2,128)(2,1)S(1)}, bf16[1,2,12,2048]{3,1,2,0:T(2,128)(2,1)S(1)}, u32[]{:S(2)}, u32[]{:S(2)}) collective-permute-start(bf16[1,2,12,2048]{3,1,2,0:T(2,128)(2,1)S(1)} %bitcast.726), channel_id=1, source_target_pairs={{0,5},{1,4},{2,7},{3,6},{4,1},{5,0},{6,3},{7,2},{8,13},{9,12},{10,... | collective-permute-start | bytes 294920 | tf_op jit(solution)/shard_map/ppermute | solution.py:26
  390.4 12.3 %collective-permute-start.37 = (bf16[1,2,12,2048]{3,1,2,0:T(2,128)(2,1)S(1)}, bf16[1,2,12,2048]{3,1,2,0:T(2,128)(2,1)S(1)}, u32[]{:S(2)}, u32[]{:S(2)}) collective-permute-start(bf16[1,2,12,2048]{3,1,2,0:T(2,128)(2,1)S(1)} %bitcast.744), channel_id=1, source_target_pairs={{0,6},{1,7},{2,4},{3,5},{4,2},{5,3},{6,0},{7,1},{8,14},{9,15},{10,... | collective-permute-start | bytes 294920 | tf_op jit(solution)/shard_map/ppermute | solution.py:26
  391.9 11.0 %collective-permute-start.38 = (bf16[1,2,12,2048]{3,1,2,0:T(2,128)(2,1)S(1)}, bf16[1,2,12,2048]{3,1,2,0:T(2,128)(2,1)S(1)}, u32[]{:S(2)}, u32[]{:S(2)}) collective-permute-start(bf16[1,2,12,2048]{3,1,2,0:T(2,128)(2,1)S(1)} %bitcast.720), channel_id=1, source_target_pairs={{0,7},{1,6},{2,5},{3,4},{4,3},{5,2},{6,1},{7,0},{8,15},{9,14},{10,... | collective-permute-start | bytes 294920 | tf_op jit(solution)/shard_map/ppermute | solution.py:26
  406.2 7.7 %collective-permute-start.39 = (bf16[16,2048]{1,0:T(8,128)(2,1)S(1)}, bf16[16,2048]{1,0:T(8,128)(2,1)S(1)}, u32[]{:S(2)}, u32[]{:S(2)}) collective-permute-start(bf16[16,2048]{1,0:T(8,128)(2,1)S(1)} %get-tuple-element.23), channel_id=1, source_target_pairs={{0,8},{8,16},{16,24},{1,9},{9,17},{17,25},{2,10},{10,18},{18,26},{... | collective-permute-start | bytes 196616 | tf_op jit(solution)/shard_map/ppermute | solution.py:34
  429.0 26.7 %all-to-all-start.5 = ((bf16[8,2,12,2048]{3,1,2,0:T(2,128)(2,1)}), bf16[8,2,12,2048]{3,1,2,0:T(2,128)(2,1)S(1)}, u32[]{:S(2)}, u32[]{:S(2)}) async-start(bf16[8,2,12,2048]{3,1,2,0:T(2,128)(2,1)} %copy.282), calls=%async_computation.5 | async-start | bytes 1572864 | tf_op jit(solution)/shard_map/all_to_all | solution.py:86
  466.7 6.0 %collective-permute-start.40 = (bf16[1,2,12,2048]{3,1,2,0:T(2,128)(2,1)S(1)}, bf16[1,2,12,2048]{3,1,2,0:T(2,128)(2,1)S(1)}, u32[]{:S(2)}, u32[]{:S(2)}) collective-permute-start(bf16[1,2,12,2048]{3,1,2,0:T(2,128)(2,1)S(1)} %bitcast.759), channel_id=1, source_target_pairs={{0,1},{1,0},{2,3},{3,2},{4,5},{5,4},{6,7},{7,6},{8,9},{9,8},{10,11... | collective-permute-start | bytes 294920 | tf_op jit(solution)/shard_map/ppermute | solution.py:26
  466.9 7.3 %collective-permute-start.41 = (bf16[1,2,12,2048]{3,1,2,0:T(2,128)(2,1)S(1)}, bf16[1,2,12,2048]{3,1,2,0:T(2,128)(2,1)S(1)}, u32[]{:S(2)}, u32[]{:S(2)}) collective-permute-start(bf16[1,2,12,2048]{3,1,2,0:T(2,128)(2,1)S(1)} %bitcast.752), channel_id=1, source_target_pairs={{0,2},{1,3},{2,0},{3,1},{4,6},{5,7},{6,4},{7,5},{8,10},{9,11},{10,... | collective-permute-start | bytes 294920 | tf_op jit(solution)/shard_map/ppermute | solution.py:26
  467.1 9.6 %collective-permute-start.42 = (bf16[1,2,12,2048]{3,1,2,0:T(2,128)(2,1)S(1)}, bf16[1,2,12,2048]{3,1,2,0:T(2,128)(2,1)S(1)}, u32[]{:S(2)}, u32[]{:S(2)}) collective-permute-start(bf16[1,2,12,2048]{3,1,2,0:T(2,128)(2,1)S(1)} %bitcast.739), channel_id=1, source_target_pairs={{0,3},{1,2},{2,1},{3,0},{4,7},{5,6},{6,5},{7,4},{8,11},{9,10},{10,... | collective-permute-start | bytes 294920 | tf_op jit(solution)/shard_map/ppermute | solution.py:26
  469.1 15.0 %collective-permute-start.43 = (bf16[1,2,12,2048]{3,1,2,0:T(2,128)(2,1)S(1)}, bf16[1,2,12,2048]{3,1,2,0:T(2,128)(2,1)S(1)}, u32[]{:S(2)}, u32[]{:S(2)}) collective-permute-start(bf16[1,2,12,2048]{3,1,2,0:T(2,128)(2,1)S(1)} %bitcast.733), channel_id=1, source_target_pairs={{0,4},{1,5},{2,6},{3,7},{4,0},{5,1},{6,2},{7,3},{8,12},{9,13},{10,... | collective-permute-start | bytes 294920 | tf_op jit(solution)/shard_map/ppermute | solution.py:26
  469.3 15.6 %collective-permute-start.44 = (bf16[1,2,12,2048]{3,1,2,0:T(2,128)(2,1)S(1)}, bf16[1,2,12,2048]{3,1,2,0:T(2,128)(2,1)S(1)}, u32[]{:S(2)}, u32[]{:S(2)}) collective-permute-start(bf16[1,2,12,2048]{3,1,2,0:T(2,128)(2,1)S(1)} %bitcast.727), channel_id=1, source_target_pairs={{0,5},{1,4},{2,7},{3,6},{4,1},{5,0},{6,3},{7,2},{8,13},{9,12},{10,... | collective-permute-start | bytes 294920 | tf_op jit(solution)/shard_map/ppermute | solution.py:26
  472.8 12.3 %collective-permute-start.45 = (bf16[1,2,12,2048]{3,1,2,0:T(2,128)(2,1)S(1)}, bf16[1,2,12,2048]{3,1,2,0:T(2,128)(2,1)S(1)}, u32[]{:S(2)}, u32[]{:S(2)}) collective-permute-start(bf16[1,2,12,2048]{3,1,2,0:T(2,128)(2,1)S(1)} %bitcast.745), channel_id=1, source_target_pairs={{0,6},{1,7},{2,4},{3,5},{4,2},{5,3},{6,0},{7,1},{8,14},{9,15},{10,... | collective-permute-start | bytes 294920 | tf_op jit(solution)/shard_map/ppermute | solution.py:26
  474.2 11.0 %collective-permute-start.46 = (bf16[1,2,12,2048]{3,1,2,0:T(2,128)(2,1)S(1)}, bf16[1,2,12,2048]{3,1,2,0:T(2,128)(2,1)S(1)}, u32[]{:S(2)}, u32[]{:S(2)}) collective-permute-start(bf16[1,2,12,2048]{3,1,2,0:T(2,128)(2,1)S(1)} %bitcast.721), channel_id=1, source_target_pairs={{0,7},{1,6},{2,5},{3,4},{4,3},{5,2},{6,1},{7,0},{8,15},{9,14},{10,... | collective-permute-start | bytes 294920 | tf_op jit(solution)/shard_map/ppermute | solution.py:26
  488.5 7.7 %collective-permute-start.47 = (bf16[16,2048]{1,0:T(8,128)(2,1)S(1)}, bf16[16,2048]{1,0:T(8,128)(2,1)S(1)}, u32[]{:S(2)}, u32[]{:S(2)}) collective-permute-start(bf16[16,2048]{1,0:T(8,128)(2,1)S(1)} %get-tuple-element.17), channel_id=1, source_target_pairs={{0,8},{8,16},{16,24},{1,9},{9,17},{17,25},{2,10},{10,18},{18,26},{... | collective-permute-start | bytes 196616 | tf_op jit(solution)/shard_map/ppermute | solution.py:34
  511.3 26.5 %all-to-all-start.6 = ((bf16[8,2,12,2048]{3,1,2,0:T(2,128)(2,1)}), bf16[8,2,12,2048]{3,1,2,0:T(2,128)(2,1)S(1)}, u32[]{:S(2)}, u32[]{:S(2)}) async-start(bf16[8,2,12,2048]{3,1,2,0:T(2,128)(2,1)} %copy.304), calls=%async_computation.6 | async-start | bytes 1572864 | tf_op jit(solution)/shard_map/all_to_all | solution.py:86
  548.8 6.0 %collective-permute-start.48 = (bf16[1,2,12,2048]{3,1,2,0:T(2,128)(2,1)S(1)}, bf16[1,2,12,2048]{3,1,2,0:T(2,128)(2,1)S(1)}, u32[]{:S(2)}, u32[]{:S(2)}) collective-permute-start(bf16[1,2,12,2048]{3,1,2,0:T(2,128)(2,1)S(1)} %bitcast.753), channel_id=1, source_target_pairs={{0,1},{1,0},{2,3},{3,2},{4,5},{5,4},{6,7},{7,6},{8,9},{9,8},{10,11... | collective-permute-start | bytes 294920 | tf_op jit(solution)/shard_map/ppermute | solution.py:26
  549.0 7.3 %collective-permute-start.49 = (bf16[1,2,12,2048]{3,1,2,0:T(2,128)(2,1)S(1)}, bf16[1,2,12,2048]{3,1,2,0:T(2,128)(2,1)S(1)}, u32[]{:S(2)}, u32[]{:S(2)}) collective-permute-start(bf16[1,2,12,2048]{3,1,2,0:T(2,128)(2,1)S(1)} %bitcast.746), channel_id=1, source_target_pairs={{0,2},{1,3},{2,0},{3,1},{4,6},{5,7},{6,4},{7,5},{8,10},{9,11},{10,... | collective-permute-start | bytes 294920 | tf_op jit(solution)/shard_map/ppermute | solution.py:26
  549.1 9.6 %collective-permute-start.50 = (bf16[1,2,12,2048]{3,1,2,0:T(2,128)(2,1)S(1)}, bf16[1,2,12,2048]{3,1,2,0:T(2,128)(2,1)S(1)}, u32[]{:S(2)}, u32[]{:S(2)}) collective-permute-start(bf16[1,2,12,2048]{3,1,2,0:T(2,128)(2,1)S(1)} %bitcast.714), channel_id=1, source_target_pairs={{0,3},{1,2},{2,1},{3,0},{4,7},{5,6},{6,5},{7,4},{8,11},{9,10},{10,... | collective-permute-start | bytes 294920 | tf_op jit(solution)/shard_map/ppermute | solution.py:26
  551.1 15.0 %collective-permute-start.51 = (bf16[1,2,12,2048]{3,1,2,0:T(2,128)(2,1)S(1)}, bf16[1,2,12,2048]{3,1,2,0:T(2,128)(2,1)S(1)}, u32[]{:S(2)}, u32[]{:S(2)}) collective-permute-start(bf16[1,2,12,2048]{3,1,2,0:T(2,128)(2,1)S(1)} %bitcast.713), channel_id=1, source_target_pairs={{0,4},{1,5},{2,6},{3,7},{4,0},{5,1},{6,2},{7,3},{8,12},{9,13},{10,... | collective-permute-start | bytes 294920 | tf_op jit(solution)/shard_map/ppermute | solution.py:26
  551.4 15.7 %collective-permute-start.52 = (bf16[1,2,12,2048]{3,1,2,0:T(2,128)(2,1)S(1)}, bf16[1,2,12,2048]{3,1,2,0:T(2,128)(2,1)S(1)}, u32[]{:S(2)}, u32[]{:S(2)}) collective-permute-start(bf16[1,2,12,2048]{3,1,2,0:T(2,128)(2,1)S(1)} %bitcast.712), channel_id=1, source_target_pairs={{0,5},{1,4},{2,7},{3,6},{4,1},{5,0},{6,3},{7,2},{8,13},{9,12},{10,... | collective-permute-start | bytes 294920 | tf_op jit(solution)/shard_map/ppermute | solution.py:26
  554.8 12.3 %collective-permute-start.53 = (bf16[1,2,12,2048]{3,1,2,0:T(2,128)(2,1)S(1)}, bf16[1,2,12,2048]{3,1,2,0:T(2,128)(2,1)S(1)}, u32[]{:S(2)}, u32[]{:S(2)}) collective-permute-start(bf16[1,2,12,2048]{3,1,2,0:T(2,128)(2,1)S(1)} %bitcast.715), channel_id=1, source_target_pairs={{0,6},{1,7},{2,4},{3,5},{4,2},{5,3},{6,0},{7,1},{8,14},{9,15},{10,... | collective-permute-start | bytes 294920 | tf_op jit(solution)/shard_map/ppermute | solution.py:26
  556.3 11.0 %collective-permute-start.54 = (bf16[1,2,12,2048]{3,1,2,0:T(2,128)(2,1)S(1)}, bf16[1,2,12,2048]{3,1,2,0:T(2,128)(2,1)S(1)}, u32[]{:S(2)}, u32[]{:S(2)}) collective-permute-start(bf16[1,2,12,2048]{3,1,2,0:T(2,128)(2,1)S(1)} %bitcast.711), channel_id=1, source_target_pairs={{0,7},{1,6},{2,5},{3,4},{4,3},{5,2},{6,1},{7,0},{8,15},{9,14},{10,... | collective-permute-start | bytes 294920 | tf_op jit(solution)/shard_map/ppermute | solution.py:26
  (1 other events, 19.6 us)
